TPU v7x, 128 devices: a whole 4x4x4 slice. The times are simulated.
128 devices in a mesh: ctx: 32 (over y, z, core), tp: 4 (over x).
Axes of the slice: x: 4, y: 4, z: 4, core: 2. Of those that a mesh axis runs over, the one named last changes fastest.
Arguments:
- hidden_in: bfloat16 [16384, 4608], P('ctx'), may hold values from -5.4 to 5.4
- pre_gain: float32 [4608], replicated, may hold values from 0.25 to 1.75
- w_query: bfloat16 [4608, 2048], P(None, 'tp'), may hold values from -0.677644 to 0.677644
- w_key: bfloat16 [4608, 1024], P(None, 'tp'), may hold values from -0.058925565 to 0.058925565
- w_value: bfloat16 [4608, 1024], P(None, 'tp'), may hold values from -0.09375 to 0.09375
- w_out: bfloat16 [2048, 4608], P('tp'), may hold values from -0.26516504 to 0.26516504
- post_gain: float32 [4608], P('tp'), may hold values from 0.25 to 1.75
Outputs:
- layer_out: bfloat16 [16384, 4608], P('ctx', 'tp')
- sink_share: float32 [16384], P('ctx')
All inputs are finite; a program needn't handle non-finite values.
Results may differ from a plain program's by a relative error of at most 0.0095.
The roundings to bfloat16 on the way count: a program that leaves them out, or rounds other values in their place, can miss the bound.
Values may be sent and summed in bfloat16 or wider, within the bound.
No kernel may reach another device: no remote copies, remote signals or barrier semaphores. Data moves between devices by JAX's collectives and lax.ppermute only.
A program may use at most 192 MiB of HBM per device.

v0:
```python
import math

import jax
import jax.numpy as jnp
from jax import lax
from jax.experimental import pallas as pl
from jax.experimental.pallas import tpu as pltpu
from jax.sharding import PartitionSpec as P


D = 4608
QHEADS = 16
HEAD = 128
WINDOW = 4096
SINKS = 4
EXP_SCALE = 50.0 / math.log(2.0)


def shifted(x, axis, by):
    devices = lax.axis_size(axis)
    pairs = [(i, i + by) for i in range(devices) if 0 <= i + by < devices]
    return lax.ppermute(x, axis, pairs)


def cyclic(x, axis, by):
    devices = lax.axis_size(axis)
    return lax.ppermute(x, axis, [(i, (i + by) % devices) for i in range(devices)])


def from_first(x, axis):
    devices = lax.axis_size(axis)
    index = lax.axis_index(axis)
    step = devices // 2
    while step >= 1:
        pairs = [(i, i + step) for i in range(0, devices, 2 * step)]
        got = lax.ppermute(x, axis, pairs)
        x = jnp.where(index % (2 * step) == step, got, x)
        step //= 2
    return x


def rope_tables(positions):
    index = jnp.arange(0, HEAD, 2).astype(jnp.float32)
    inverse = jnp.exp(-jnp.log(jnp.float32(10000.0)) * index / HEAD)
    angles = positions.astype(jnp.float32)[:, None] * inverse[None, :]
    angles = jnp.concatenate([angles, angles], axis=1)
    return (jnp.cos(angles)[:, None, :], jnp.sin(angles)[:, None, :])


def rotate(values, cosine_table, sine_table):
    half = values.shape[-1] // 2
    turned = jnp.concatenate([-values[..., half:], values[..., :half]], axis=-1)
    return values * cosine_table + turned * sine_table


def window_attention(query, cosine, sine, pieces, orders, sink_pad, offset, local_kv, group, extra=(), tq=256, chunk=256):
    tok_rows = query.shape[0]
    n_qt = tok_rows // tq
    piece_rows = pieces[0].shape[0]
    n_pieces = len(pieces)
    span = piece_rows * len(orders[0])
    rows = group * tq
    win = WINDOW + tq
    nchunks = win // chunk
    pad_rows = sink_pad.shape[0]

    def kernel(off_ref, q_ref, cos_ref, sin_ref, sk_ref, sv_ref, *rest):
        piece_refs = rest[:n_pieces]
        o_ref, ss_ref, expo_scr, acc_scr, rs_scr, k_ref, v_ref, w_scr, sems = rest[n_pieces + len(extra):]
        k = pl.program_id(0)
        i = pl.program_id(1)

        parity = (off_ref[0] // piece_rows) % len(orders)

        def fetch(order):
            copies = []
            for p, src in enumerate(order):
                rows_p = pl.ds(p * piece_rows, piece_rows)
                copies.append(pltpu.make_async_copy(
                    piece_refs[src].at[:, pl.ds(k * HEAD, HEAD)], k_ref.at[rows_p, :], sems.at[0, p]))
                copies.append(pltpu.make_async_copy(
                    piece_refs[src].at[:, pl.ds((local_kv + k) * HEAD, HEAD)], v_ref.at[rows_p, :], sems.at[1, p]))
            for cp in copies:
                cp.start()
            for cp in copies:
                cp.wait()

        for which, order in enumerate(orders):
            pl.when((i == 0) & (parity == which))(lambda order=order: fetch(order))

        q0 = i * tq
        base = off_ref[0] - WINDOW + q0
        half = lax.broadcasted_iota(jnp.int32, (1, HEAD), 1) < HEAD // 2
        sign = jnp.where(half, -1.0, 1.0).astype(jnp.float32)
        cos_t = cos_ref[...]
        sin_t = sin_ref[...]
        heads = []
        for g in range(group):
            x = q_ref[:, g * HEAD:(g + 1) * HEAD]
            turned = pltpu.roll(x, HEAD // 2, 1) * sign
            heads.append((x * cos_t + turned * sin_t).astype(jnp.bfloat16))
        q = jnp.concatenate(heads, axis=0)
        qi = lax.broadcasted_iota(jnp.int32, (rows, 1), 0) % tq
        lo = jnp.maximum(qi + 1, SINKS - base)
        hi = qi + WINDOW
        first = jnp.maximum(SINKS - base, 0) // chunk
        rs_scr[...] = jnp.zeros((rows, 128), jnp.float32)

        def keep(c, e):
            expo_scr[c] = e
            part = e[:, 0:128]
            for h in range(1, chunk // 128):
                part = part + e[:, h * 128:(h + 1) * 128]
            rs_scr[...] += part

        def squash(c):
            start = pl.multiple_of(q0 + c * chunk, chunk)
            kc = k_ref[pl.ds(start, chunk), :]
            s = lax.dot_general(q, kc, (((1,), (1,)), ((), ())), preferred_element_type=jnp.float32)
            return jnp.tanh(s * (1.0 / 600.0))

        def pass1(c, carry):
            edge = (c * chunk < tq) | ((c + 1) * chunk > WINDOW + 1) | (base + c * chunk < SINKS)

            @pl.when(edge)
            def _():
                u = squash(c)
                col = c * chunk + lax.broadcasted_iota(jnp.int32, (1, chunk), 1)
                live = (col >= lo) & (col <= hi)
                keep(c, jnp.where(live, jnp.exp2(u * EXP_SCALE), 0.0))

            @pl.when(jnp.logical_not(edge))
            def _():
                keep(c, jnp.exp2(squash(c) * EXP_SCALE))

            return carry

        lax.fori_loop(first, nchunks, pass1, 0)
        rowsum = jnp.sum(rs_scr[...], axis=1, keepdims=True)
        ssc = lax.dot_general(q, sk_ref[...], (((1,), (1,)), ((), ())), preferred_element_type=jnp.float32)
        su = jnp.tanh(ssc * (1.0 / 600.0))
        scol = lax.broadcasted_iota(jnp.int32, (1, pad_rows), 1)
        qpos = off_ref[0] + q0 + qi
        slive = (scol < SINKS) & (qpos >= scol)
        se = jnp.where(slive, jnp.exp2(su * EXP_SCALE), 0.0)
        ssum = jnp.sum(se, axis=1, keepdims=True)
        total = rowsum + ssum
        inv = 1.0 / total
        sw = (se * inv).astype(jnp.bfloat16)
        acc_scr[...] = jnp.dot(sw, sv_ref[...], preferred_element_type=jnp.float32)

        def pass2(c, carry):
            cols = pl.ds(pl.multiple_of(c * chunk, chunk), chunk)

            @pl.when(c < first)
            def _():
                w_scr[:, cols] = jnp.zeros((rows, chunk), jnp.bfloat16)

            @pl.when(c >= first)
            def _():
                w_scr[:, cols] = (expo_scr[c] * inv).astype(jnp.bfloat16)

            return carry

        lax.fori_loop(0, nchunks, pass2, 0)
        vw = v_ref[pl.ds(pl.multiple_of(q0, chunk), win), :]
        out = acc_scr[...] + jnp.dot(w_scr[...], vw, preferred_element_type=jnp.float32)
        out16 = out.astype(jnp.bfloat16)
        for g in range(group):
            o_ref[:, g * HEAD:(g + 1) * HEAD] = out16[g * tq:(g + 1) * tq]
            ss_ref[0, g] = ssum[g * tq:(g + 1) * tq]

    off = jnp.reshape(offset, (1,)).astype(jnp.int32)
    return pl.pallas_call(
        kernel,
        out_shape=(
            jax.ShapeDtypeStruct((tok_rows, local_kv * group * HEAD), jnp.bfloat16),
            jax.ShapeDtypeStruct((local_kv, group, tok_rows, 1), jnp.float32),
        ),
        grid_spec=pltpu.PrefetchScalarGridSpec(
            num_scalar_prefetch=1,
            grid=(local_kv, n_qt),
            in_specs=[
                pl.BlockSpec((tq, group * HEAD), lambda k, i, o: (i, k)),
                pl.BlockSpec((tq, HEAD), lambda k, i, o: (i, 0)),
                pl.BlockSpec((tq, HEAD), lambda k, i, o: (i, 0)),
                pl.BlockSpec((pad_rows, HEAD), lambda k, i, o: (0, k)),
                pl.BlockSpec((pad_rows, HEAD), lambda k, i, o: (0, local_kv + k)),
            ] + [pl.BlockSpec(memory_space=pl.ANY) for _ in tuple(pieces) + tuple(extra)],
            out_specs=[
                pl.BlockSpec((tq, group * HEAD), lambda k, i, o: (i, k)),
                pl.BlockSpec((1, group, tq, 1), lambda k, i, o: (k, 0, i, 0)),
            ],
            scratch_shapes=[
                pltpu.VMEM((nchunks, rows, chunk), jnp.float32),
                pltpu.VMEM((rows, HEAD), jnp.float32),
                pltpu.VMEM((rows, 128), jnp.float32),
                pltpu.VMEM((span, HEAD), jnp.bfloat16),
                pltpu.VMEM((span, HEAD), jnp.bfloat16),
                pltpu.VMEM((rows, win), jnp.bfloat16),
                pltpu.SemaphoreType.DMA((2, len(orders[0]))),
            ],
        ),
        compiler_params=pltpu.CompilerParams(dimension_semantics=("arbitrary", "arbitrary")),
    )(off, query, cosine, sine, sink_pad, sink_pad, *pieces, *extra)


def on_device(hidden_in, pre_gain, w_query, w_key, w_value, w_out, post_gain):
    tok_rows = hidden_in.shape[0]
    local_q = w_query.shape[1] // HEAD
    local_kv = w_key.shape[1] // HEAD
    group = local_q // local_kv
    tp_n = lax.axis_size("tp")
    tp_i = lax.axis_index("tp")
    cols_dev = post_gain.shape[0]

    w_recv = []
    for k in range(tp_n):
        part = lax.dynamic_slice_in_dim(w_out, ((tp_i + k) % tp_n) * cols_dev, cols_dev, 1)
        w_recv.append(part if k == 0 else cyclic(part, "tp", k))

    offset = lax.axis_index("ctx") * tok_rows
    inputs = hidden_in.astype(jnp.float32)
    normed = (
        inputs * lax.rsqrt(jnp.mean(inputs * inputs, axis=-1, keepdims=True) + 1e-06) * pre_gain
    ).astype(jnp.bfloat16)
    positions = offset + jnp.arange(tok_rows, dtype=jnp.int32)
    cosine_table, sine_table = rope_tables(positions)
    query = jnp.dot(normed, w_query, preferred_element_type=jnp.float32)
    keys = jnp.dot(normed, w_key, preferred_element_type=jnp.float32).reshape(tok_rows, -1, HEAD)
    keys = rotate(keys, cosine_table, sine_table).astype(jnp.bfloat16).reshape(tok_rows, -1)
    values = jnp.dot(normed, w_value, preferred_element_type=jnp.float32).astype(jnp.bfloat16)
    kv = jnp.concatenate([keys, values], axis=1)

    sink_kv = from_first(kv[:SINKS], "ctx")
    sink_pad = jnp.zeros((HEAD, sink_kv.shape[1]), sink_kv.dtype).at[:SINKS].set(sink_kv)
    reach = WINDOW // tok_rows
    pieces = [shifted(kv, "ctx", distance) for distance in range(reach, 0, -1)] + [kv]
    orders = (tuple(range(len(pieces))),)
    attended, sink_parts = window_attention(
        query, cosine_table[:, 0, :], sine_table[:, 0, :], pieces, orders, sink_pad, offset, local_kv, group,
        extra=tuple(w_recv[1:]),
    )
    sink_sums = jnp.sum(sink_parts[..., 0], axis=(0, 1))
    projected = jnp.dot(attended, w_recv[0], preferred_element_type=jnp.float32)
    for k in range(1, tp_n):
        projected = projected + jnp.dot(
            cyclic(attended, "tp", k), w_recv[k], preferred_element_type=jnp.float32
        )
    squares = jnp.sum(projected * projected, axis=-1)
    total_squares, total_sinks = lax.psum((squares, sink_sums), "tp")
    post = projected * lax.rsqrt(total_squares / D + 1e-06)[:, None] * post_gain
    own_cols = lax.dynamic_slice_in_dim(hidden_in, tp_i * cols_dev, cols_dev, 1).astype(jnp.float32)
    layer_out = (own_cols + post).astype(jnp.bfloat16)
    sink_share = jnp.log(total_sinks / QHEADS)
    return (layer_out, sink_share)


def solution(mesh):
    return jax.shard_map(
        on_device,
        mesh=mesh,
        in_specs=(
            P("ctx", None),
            P(),
            P(None, "tp"),
            P(None, "tp"),
            P(None, "tp"),
            P("tp", None),
            P("tp"),
        ),
        out_specs=(P("ctx", "tp"), P("ctx")),
        check_vma=False,
    )
```

profile of v0, /device:TPU:8, one launch (start us, length us, event | category | flops | bytes accessed | tf_op | source)
XLA Modules:
  0.0 213.5 jit_solution(12670484036030911734)
XLA Ops:
  2.0 3.6 %fusion = f32[512]{0:T(512)S(1)} fusion(bf16[512,4608]{1,0:T(8,128)(2,1)} %param.9), kind=kLoop, calls=%fused_computation.2 | loop fusion | flops 7077376 | bytes 4720640 | tf_op jit(solution)/shard_map/reduce_sum | solution.py:225
  6.0 2.6 %fusion.12 = f32[512,256]{0,1:T(8,128)} fusion(bf16[4608,256]{1,0:T(8,128)(2,1)S(1)} %copy-done, bf16[512,4608]{1,0:T(8,128)(2,1)S(1)} %copy-done.1, f32[4608]{0:T(1024)S(1)} %copy-done.12, f32[512]{0:T(512)S(1)} %add_rsqrt_fusion.1), kind=kOutput, calls=%fused_computation.38 | convolution fusion | flops 1217396736 | bytes 7622656 | tf_op jit(solution)/shard_map/dot_general | solution.py:230
  17.7 4.6 %convolution_convert_fusion = bf16[512,256]{1,0:T(8,128)(2,1)S(1)} fusion(bf16[4608,256]{1,0:T(8,128)(2,1)} %param.13, bf16[512,4608]{1,0:T(8,128)(2,1)} %param.9, f32[4608]{0:T(1024)S(1)} %copy-done.12, f32[512]{0:T(512)S(1)} %add_rsqrt_fusion.1), kind=kOutput, calls=%fused_computation.10 | convolution fusion | flops 1217527808 | bytes 7360512 | tf_op jit(solution)/shard_map/dot_general | solution.py:232
  27.1 2.6 %collective-permute-start.10 = (bf16[512,512]{1,0:T(8,128)(2,1)}, bf16[512,512]{1,0:T(8,128)(2,1)S(1)}, u32[]{:S(2)}, u32[]{:S(2)}) collective-permute-start(bf16[512,512]{1,0:T(8,128)(2,1)} %pad_maximum_fusion.rest_8_), channel_id=1, source_target_pairs={{0,12},{4,16},{8,20},{12,24},{16,28},{20,32},{24,36},{28,40},{32,4... | collective-permute-start | bytes 1572872 | tf_op jit(solution)/shard_map/ppermute | solution.py:22
  29.8 3.3 %collective-permute-done.1 = bf16[4,512]{1,0:T(4,128)(2,1)S(1)} collective-permute-done((bf16[4,512]{1,0:T(4,128)(2,1)S(1)}, bf16[4,512]{1,0:T(4,128)(2,1)S(1)}, u32[]{:S(2)}, u32[]{:S(2)}) %collective-permute-start.1) | collective-permute-done | bytes 4128 | tf_op jit(solution)/shard_map/ppermute | solution.py:36
  35.3 5.1 %collective-permute-done.2 = bf16[4,512]{1,0:T(4,128)(2,1)S(1)} collective-permute-done((bf16[4,512]{1,0:T(4,128)(2,1)S(1)}, bf16[4,512]{1,0:T(4,128)(2,1)S(1)}, u32[]{:S(2)}, u32[]{:S(2)}) %collective-permute-start.2) | collective-permute-done | bytes 4128 | tf_op jit(solution)/shard_map/ppermute | solution.py:36
  45.6 11.0 %collective-permute-start.5 = (bf16[512,512]{1,0:T(8,128)(2,1)}, bf16[512,512]{1,0:T(8,128)(2,1)}, u32[]{:S(2)}, u32[]{:S(2)}) collective-permute-start(bf16[512,512]{1,0:T(8,128)(2,1)} %pad_maximum_fusion.rest_8_), channel_id=1, source_target_pairs={{0,32},{4,36},{8,40},{12,44},{16,48},{20,52},{24,56},{28,60},{32,6... | collective-permute-start | bytes 1572872 | tf_op jit(solution)/shard_map/ppermute | solution.py:22
  56.6 5.7 %collective-permute-start.4 = (bf16[4,512]{1,0:T(4,128)(2,1)S(1)}, bf16[4,512]{1,0:T(4,128)(2,1)S(1)}, u32[]{:S(2)}, u32[]{:S(2)}) collective-permute-start(bf16[4,512]{1,0:T(4,128)(2,1)S(1)} %broadcast_select_fusion.3), channel_id=1, source_target_pairs={{0,4},{8,12},{16,20},{24,28},{32,36},{40,44},{48,52},{56,60},{64,6... | collective-permute-start | bytes 12296 | tf_op jit(solution)/shard_map/ppermute | solution.py:36
  67.0 3.9 %constant_dynamic-slice_fusion = (bf16[512,1152]{1,0:T(8,128)(2,1)}, bf16[512,1152]{1,0:T(8,128)(2,1)}, bf16[512,1152]{1,0:T(8,128)(2,1)}) fusion(bf16[512,4608]{1,0:T(8,128)(2,1)} %param.14, s32[]{:T(128)S(6)} %select_n.107, s32[]{:T(128)S(6)} %select_n.105, s32[]{:T(128)S(6)} %select_n.103), kind=kLoop, calls=%fused_computation.34 | loop fusion | bytes 7077900 | tf_op jit(solution)/shard_map/dynamic_slice | solution.py:219
  73.2 2.7 %collective-permute-start.14 = (bf16[512,1152]{1,0:T(8,128)(2,1)}, bf16[512,1152]{1,0:T(8,128)(2,1)}, u32[]{:S(2)}, u32[]{:S(2)}) collective-permute-start(bf16[512,1152]{1,0:T(8,128)(2,1)} %get-tuple-element.21), channel_id=1, source_target_pairs={{0,2},{1,3},{2,0},{3,1},{4,6},{5,7},{6,4},{7,5},{8,10},{9,11},{10,... | collective-permute-start | bytes 3538952 | tf_op jit(solution)/shard_map/ppermute | solution.py:27
  77.4 10.6 %collective-permute-start.8 = (bf16[512,512]{1,0:T(8,128)(2,1)}, bf16[512,512]{1,0:T(8,128)(2,1)}, u32[]{:S(2)}, u32[]{:S(2)}) collective-permute-start(bf16[512,512]{1,0:T(8,128)(2,1)} %pad_maximum_fusion.rest_8_), channel_id=1, source_target_pairs={{0,20},{4,24},{8,28},{12,32},{16,36},{20,40},{24,44},{28,48},{32,5... | collective-permute-start | bytes 1572872 | tf_op jit(solution)/shard_map/ppermute | solution.py:22
  88.0 4.5 %collective-permute-done.7.rest_2_ = bf16[512,512]{1,0:T(8,128)(2,1)} collective-permute-done((bf16[512,512]{1,0:T(8,128)(2,1)}, bf16[512,512]{1,0:T(8,128)(2,1)}, u32[]{:S(2)}, u32[]{:S(2)}) %collective-permute-start.7) | collective-permute-done | bytes 524320 | tf_op jit(solution)/shard_map/ppermute | solution.py:22
  92.5 7.3 %collective-permute-start.9 = (bf16[512,512]{1,0:T(8,128)(2,1)}, bf16[512,512]{1,0:T(8,128)(2,1)}, u32[]{:S(2)}, u32[]{:S(2)}) collective-permute-start(bf16[512,512]{1,0:T(8,128)(2,1)} %pad_maximum_fusion.rest_8_), channel_id=1, source_target_pairs={{0,16},{4,20},{8,24},{12,28},{16,32},{20,36},{24,40},{28,44},{32,4... | collective-permute-start | bytes 1572872 | tf_op jit(solution)/shard_map/ppermute | solution.py:22
  99.8 7.4 %fusion.14.q_ref = f32[512,512]{1,0:T(8,128)} fusion(bf16[4608,512]{1,0:T(8,128)(2,1)} %param.11, bf16[512,4608]{1,0:T(8,128)(2,1)} %param.9, f32[4608]{0:T(1024)S(1)} %copy-done.13, f32[512]{0:T(512)S(1)} %add_rsqrt_fusion.1), kind=kOutput, calls=%fused_computation.39 | convolution fusion | flops 2425356288 | bytes 10506240 | tf_op jit(solution)/shard_map/dot_general | solution.py:229
  107.9 6.8 %collective-permute-done.9.rest_4_ = bf16[512,512]{1,0:T(8,128)(2,1)} collective-permute-done((bf16[512,512]{1,0:T(8,128)(2,1)}, bf16[512,512]{1,0:T(8,128)(2,1)}, u32[]{:S(2)}, u32[]{:S(2)}) %collective-permute-start.9) | collective-permute-done | bytes 524320 | tf_op jit(solution)/shard_map/ppermute | solution.py:22
  114.7 13.1 %collective-permute-done.14.rest_10_ = bf16[512,1152]{1,0:T(8,128)(2,1)} collective-permute-done((bf16[512,1152]{1,0:T(8,128)(2,1)}, bf16[512,1152]{1,0:T(8,128)(2,1)}, u32[]{:S(2)}, u32[]{:S(2)}) %collective-permute-start.14) | collective-permute-done | bytes 1179680 | tf_op jit(solution)/shard_map/ppermute | solution.py:27
  127.8 38.5 %shard_map.86 = (bf16[512,512]{1,0:T(8,128)(2,1)}, f32[2,2,512,1]{3,2,1,0:T(8,128)}) custom-call(s32[1]{0:T(128)} %bitcast.off_ref, f32[512,512]{1,0:T(8,128)} %fusion.14.q_ref, f32[512,128]{1,0:T(8,128)} %copy-done.4, f32[512,128]{1,0:T(8,128)} %copy-done.3, bf16[128,512]{1,0:T(8,128)(2,1)} %scatter.4.sk_ref.sv_ref, bf16[128,512]{1,0:T(8,128)(2,1)} %scatter.4.sk_ref.sv_ref, ...), custom_call_target="tpu_custom_call" | custom-call | tf_op jit(solution)/shard_map/pallas_call | solution.py:174
  167.7 2.3 %collective-permute-start.17 = (bf16[512,512]{1,0:T(8,128)(2,1)}, bf16[512,512]{1,0:T(8,128)(2,1)S(1)}, u32[]{:S(2)}, u32[]{:S(2)}) collective-permute-start(bf16[512,512]{1,0:T(8,128)(2,1)} %get-tuple-element.16), channel_id=1, source_target_pairs={{0,2},{1,3},{2,0},{3,1},{4,6},{5,7},{6,4},{7,5},{8,10},{9,11},{10,... | collective-permute-start | bytes 1572872 | tf_op jit(solution)/shard_map/ppermute | solution.py:27
  173.1 8.1 %collective-permute-done.16 = bf16[512,512]{1,0:T(8,128)(2,1)S(1)} collective-permute-done((bf16[512,512]{1,0:T(8,128)(2,1)}, bf16[512,512]{1,0:T(8,128)(2,1)S(1)}, u32[]{:S(2)}, u32[]{:S(2)}) %collective-permute-start.16) | collective-permute-done | bytes 524320 | tf_op jit(solution)/shard_map/ppermute | solution.py:27
  183.2 10.1 %collective-permute-done.17 = bf16[512,512]{1,0:T(8,128)(2,1)S(1)} collective-permute-done((bf16[512,512]{1,0:T(8,128)(2,1)}, bf16[512,512]{1,0:T(8,128)(2,1)S(1)}, u32[]{:S(2)}, u32[]{:S(2)}) %collective-permute-start.17) | collective-permute-done | bytes 524320 | tf_op jit(solution)/shard_map/ppermute | solution.py:27
  195.5 2.3 %fusion.19 = f32[512,1152]{1,0:T(8,128)S(1)} fusion(bf16[512,512]{1,0:T(8,128)(2,1)} %collective-permute-done.18, bf16[512,1152]{1,0:T(8,128)(2,1)} %collective-permute-done.15.rest_11_), kind=kOutput, calls=%fused_computation.43 | convolution fusion | flops 603979776 | bytes 4063232 | tf_op jit(solution)/shard_map/dot_general | solution.py:247
  197.9 3.8 %multiply_reduce_fusion = (f32[512]{0:T(512)S(1)}, f32[512,1152]{1,0:T(8,128)}) fusion(f32[512,1152]{1,0:T(8,128)S(1)} %fusion.19, f32[512,1152]{1,0:T(8,128)S(1)} %fusion.18, f32[512,1152]{1,0:T(8,128)S(1)} %fusion.17, bf16[512,512]{1,0:T(8,128)(2,1)S(1)} %copy-done.10, bf16[512,4608]{1,0:T(8,128)(2,1)} %param.14, s32[]{:T(128)S(6)} %select_n.109), kind=kOutput, calls=%fused_computation.9 | convolution fusion | flops 606928384 | bytes 11143172 | tf_op jit(solution)/shard_map/dot_general | solution.py:245
  201.6 7.9 %all-reduce.1 = (f32[512]{0:T(512)S(1)}, f32[512]{0:T(512)S(1)}) all-reduce(f32[512]{0:T(512)S(1)} %get-tuple-element.27, f32[512]{0:T(512)S(1)} %reduce_sum.29), channel_id=1, replica_groups=mesh['ctx'=32,'tp'=4] {'tp'}, use_global_device_ids=true, to_apply=%region_2.3 | all-reduce | flops 1024 | bytes 8192 | tf_op jit(solution)/shard_map/psum | solution.py:251
  210.1 3.4 %add_convert_fusion = bf16[512,1152]{1,0:T(8,128)(2,1)} fusion(f32[512,1152]{1,0:T(8,128)} %get-tuple-element.28, f32[1152]{0:T(1024)S(1)} %copy-done.11, f32[512]{0:T(512)S(1)} %get-tuple-element.30, bf16[512,4608]{1,0:T(8,128)(2,1)} %param.9, s32[]{:T(128)S(6)} %select_n.86), kind=kLoop, calls=%fused_computation.8 | loop fusion | flops 2949120 | bytes 4725252 | tf_op jit(solution)/shard_map/convert_element_type | solution.py:254
  (77 shorter events, 41.3 us)
Async XLA Ops:
  2.0 20.3 %copy-start.3 = (f32[512,128]{1,0:T(8,128)}, f32[512,128]{1,0:T(8,128)S(1)}, u32[]{:S(2)}) copy-start(f32[512,128]{1,0:T(8,128)S(1)} %get-tuple-element.25.sin_ref) | copy-start | bytes 786436
  2.0 21.0 %copy-start.4 = (f32[512,128]{1,0:T(8,128)}, f32[512,128]{1,0:T(8,128)S(1)}, u32[]{:S(2)}) copy-start(f32[512,128]{1,0:T(8,128)S(1)} %get-tuple-element.26.cos_ref) | copy-start | bytes 786436
  23.3 0.7 collective-permute-start
  24.0 9.0 %collective-permute-start.1 = (bf16[4,512]{1,0:T(4,128)(2,1)S(1)}, bf16[4,512]{1,0:T(4,128)(2,1)S(1)}, u32[]{:S(2)}, u32[]{:S(2)}) collective-permute-start(bf16[4,512]{1,0:T(4,128)(2,1)S(1)} %broadcast_select_fusion), channel_id=1, source_target_pairs={{0,32},{64,96},{1,33},{65,97},{2,34},{66,98},{3,35},{67,99}} | collective-permute-start | bytes 12296 | tf_op jit(solution)/shard_map/ppermute | solution.py:36
  27.1 37.9 %collective-permute-start.10 = (bf16[512,512]{1,0:T(8,128)(2,1)}, bf16[512,512]{1,0:T(8,128)(2,1)S(1)}, u32[]{:S(2)}, u32[]{:S(2)}) collective-permute-start(bf16[512,512]{1,0:T(8,128)(2,1)} %pad_maximum_fusion.rest_8_), channel_id=1, source_target_pairs={{0,12},{4,16},{8,20},{12,24},{16,28},{20,32},{24,36},{28,40},{32,4... | collective-permute-start | bytes 1572872 | tf_op jit(solution)/shard_map/ppermute | solution.py:22
  33.1 7.4 %collective-permute-start.2 = (bf16[4,512]{1,0:T(4,128)(2,1)S(1)}, bf16[4,512]{1,0:T(4,128)(2,1)S(1)}, u32[]{:S(2)}, u32[]{:S(2)}) collective-permute-start(bf16[4,512]{1,0:T(4,128)(2,1)S(1)} %broadcast_select_fusion.1), channel_id=1, source_target_pairs={{0,16},{32,48},{64,80},{96,112},{1,17},{33,49},{65,81},{97,113},{2... | collective-permute-start | bytes 12296 | tf_op jit(solution)/shard_map/ppermute | solution.py:36
  40.5 16.2 %collective-permute-start.3 = (bf16[4,512]{1,0:T(4,128)(2,1)S(1)}, bf16[4,512]{1,0:T(4,128)(2,1)S(1)}, u32[]{:S(2)}, u32[]{:S(2)}) collective-permute-start(bf16[4,512]{1,0:T(4,128)(2,1)S(1)} %broadcast_select_fusion.2), channel_id=1, source_target_pairs={{0,8},{16,24},{32,40},{48,56},{64,72},{80,88},{96,104},{112,120},{... | collective-permute-start | bytes 12296 | tf_op jit(solution)/shard_map/ppermute | solution.py:36
  41.7 29.2 %collective-permute-start.11 = (bf16[512,512]{1,0:T(8,128)(2,1)}, bf16[512,512]{1,0:T(8,128)(2,1)S(1)}, u32[]{:S(2)}, u32[]{:S(2)}) collective-permute-start(bf16[512,512]{1,0:T(8,128)(2,1)} %pad_maximum_fusion.rest_8_), channel_id=1, source_target_pairs={{0,8},{4,12},{8,16},{12,20},{16,24},{20,28},{24,32},{28,36},{32,40... | collective-permute-start | bytes 1572872 | tf_op jit(solution)/shard_map/ppermute | solution.py:22
  43.7 29.5 %collective-permute-start.12 = (bf16[512,512]{1,0:T(8,128)(2,1)}, bf16[512,512]{1,0:T(8,128)(2,1)}, u32[]{:S(2)}, u32[]{:S(2)}) collective-permute-start(bf16[512,512]{1,0:T(8,128)(2,1)} %pad_maximum_fusion.rest_8_), channel_id=1, source_target_pairs={{0,4},{4,8},{8,12},{12,16},{16,20},{20,24},{24,28},{28,32},{32,36}... | collective-permute-start | bytes 1572872 | tf_op jit(solution)/shard_map/ppermute | solution.py:22
  45.6 30.4 %collective-permute-start.5 = (bf16[512,512]{1,0:T(8,128)(2,1)}, bf16[512,512]{1,0:T(8,128)(2,1)}, u32[]{:S(2)}, u32[]{:S(2)}) collective-permute-start(bf16[512,512]{1,0:T(8,128)(2,1)} %pad_maximum_fusion.rest_8_), channel_id=1, source_target_pairs={{0,32},{4,36},{8,40},{12,44},{16,48},{20,52},{24,56},{28,60},{32,6... | collective-permute-start | bytes 1572872 | tf_op jit(solution)/shard_map/ppermute | solution.py:22
  56.6 6.5 %collective-permute-start.4 = (bf16[4,512]{1,0:T(4,128)(2,1)S(1)}, bf16[4,512]{1,0:T(4,128)(2,1)S(1)}, u32[]{:S(2)}, u32[]{:S(2)}) collective-permute-start(bf16[4,512]{1,0:T(4,128)(2,1)S(1)} %broadcast_select_fusion.3), channel_id=1, source_target_pairs={{0,4},{8,12},{16,20},{24,28},{32,36},{40,44},{48,52},{56,60},{64,6... | collective-permute-start | bytes 12296 | tf_op jit(solution)/shard_map/ppermute | solution.py:36
  63.1 14.3 %collective-permute-start.6 = (bf16[512,512]{1,0:T(8,128)(2,1)}, bf16[512,512]{1,0:T(8,128)(2,1)}, u32[]{:S(2)}, u32[]{:S(2)}) collective-permute-start(bf16[512,512]{1,0:T(8,128)(2,1)} %pad_maximum_fusion.rest_8_), channel_id=1, source_target_pairs={{0,28},{4,32},{8,36},{12,40},{16,44},{20,48},{24,52},{28,56},{32,6... | collective-permute-start | bytes 1572872 | tf_op jit(solution)/shard_map/ppermute | solution.py:22
  65.1 27.5 %collective-permute-start.7 = (bf16[512,512]{1,0:T(8,128)(2,1)}, bf16[512,512]{1,0:T(8,128)(2,1)}, u32[]{:S(2)}, u32[]{:S(2)}) collective-permute-start(bf16[512,512]{1,0:T(8,128)(2,1)} %pad_maximum_fusion.rest_8_), channel_id=1, source_target_pairs={{0,24},{4,28},{8,32},{12,36},{16,40},{20,44},{24,48},{28,52},{32,5... | collective-permute-start | bytes 1572872 | tf_op jit(solution)/shard_map/ppermute | solution.py:22
  67.0 32.8 %copy-start.13 = (f32[4608]{0:T(1024)S(1)}, f32[4608]{0:T(1024)}, u32[]{:S(2)}) copy-start(f32[4608]{0:T(1024)} %param.10) | copy-start | bytes 55300
  71.7 43.0 %collective-permute-start.13 = (bf16[512,1152]{1,0:T(8,128)(2,1)}, bf16[512,1152]{1,0:T(8,128)(2,1)S(1)}, u32[]{:S(2)}, u32[]{:S(2)}) collective-permute-start(bf16[512,1152]{1,0:T(8,128)(2,1)} %get-tuple-element.22), channel_id=1, source_target_pairs={{0,1},{1,2},{2,3},{3,0},{4,5},{5,6},{6,7},{7,4},{8,9},{9,10},{10,1... | collective-permute-start | bytes 3538952 | tf_op jit(solution)/shard_map/ppermute | solution.py:27
  73.2 54.6 %collective-permute-start.14 = (bf16[512,1152]{1,0:T(8,128)(2,1)}, bf16[512,1152]{1,0:T(8,128)(2,1)}, u32[]{:S(2)}, u32[]{:S(2)}) collective-permute-start(bf16[512,1152]{1,0:T(8,128)(2,1)} %get-tuple-element.21), channel_id=1, source_target_pairs={{0,2},{1,3},{2,0},{3,1},{4,6},{5,7},{6,4},{7,5},{8,10},{9,11},{10,... | collective-permute-start | bytes 3538952 | tf_op jit(solution)/shard_map/ppermute | solution.py:27
  75.9 51.8 %collective-permute-start.15 = (bf16[512,1152]{1,0:T(8,128)(2,1)}, bf16[512,1152]{1,0:T(8,128)(2,1)}, u32[]{:S(2)}, u32[]{:S(2)}) collective-permute-start(bf16[512,1152]{1,0:T(8,128)(2,1)} %get-tuple-element.20), channel_id=1, source_target_pairs={{0,3},{1,0},{2,1},{3,2},{4,7},{5,4},{6,5},{7,6},{8,11},{9,8},{10,9... | collective-permute-start | bytes 3538952 | tf_op jit(solution)/shard_map/ppermute | solution.py:27
  77.4 30.5 %collective-permute-start.8 = (bf16[512,512]{1,0:T(8,128)(2,1)}, bf16[512,512]{1,0:T(8,128)(2,1)}, u32[]{:S(2)}, u32[]{:S(2)}) collective-permute-start(bf16[512,512]{1,0:T(8,128)(2,1)} %pad_maximum_fusion.rest_8_), channel_id=1, source_target_pairs={{0,20},{4,24},{8,28},{12,32},{16,36},{20,40},{24,44},{28,48},{32,5... | collective-permute-start | bytes 1572872 | tf_op jit(solution)/shard_map/ppermute | solution.py:22
  92.5 22.2 %collective-permute-start.9 = (bf16[512,512]{1,0:T(8,128)(2,1)}, bf16[512,512]{1,0:T(8,128)(2,1)}, u32[]{:S(2)}, u32[]{:S(2)}) collective-permute-start(bf16[512,512]{1,0:T(8,128)(2,1)} %pad_maximum_fusion.rest_8_), channel_id=1, source_target_pairs={{0,16},{4,20},{8,24},{12,28},{16,32},{20,36},{24,40},{28,44},{32,4... | collective-permute-start | bytes 1572872 | tf_op jit(solution)/shard_map/ppermute | solution.py:22
  114.7 13.1 %copy-start.2 = (bf16[512,1152]{1,0:T(8,128)(2,1)}, bf16[512,1152]{1,0:T(8,128)(2,1)S(1)}, u32[]{:S(2)}) copy-start(bf16[512,1152]{1,0:T(8,128)(2,1)S(1)} %collective-permute-done.13.rest_9_) | copy-start | bytes 3538948
  166.3 14.9 %collective-permute-start.16 = (bf16[512,512]{1,0:T(8,128)(2,1)}, bf16[512,512]{1,0:T(8,128)(2,1)S(1)}, u32[]{:S(2)}, u32[]{:S(2)}) collective-permute-start(bf16[512,512]{1,0:T(8,128)(2,1)} %get-tuple-element.16), channel_id=1, source_target_pairs={{0,1},{1,2},{2,3},{3,0},{4,5},{5,6},{6,7},{7,4},{8,9},{9,10},{10,1... | collective-permute-start | bytes 1572872 | tf_op jit(solution)/shard_map/ppermute | solution.py:27
  167.7 25.6 %collective-permute-start.17 = (bf16[512,512]{1,0:T(8,128)(2,1)}, bf16[512,512]{1,0:T(8,128)(2,1)S(1)}, u32[]{:S(2)}, u32[]{:S(2)}) collective-permute-start(bf16[512,512]{1,0:T(8,128)(2,1)} %get-tuple-element.16), channel_id=1, source_target_pairs={{0,2},{1,3},{2,0},{3,1},{4,6},{5,7},{6,4},{7,5},{8,10},{9,11},{10,... | collective-permute-start | bytes 1572872 | tf_op jit(solution)/shard_map/ppermute | solution.py:27
  170.1 25.4 %collective-permute-start.18 = (bf16[512,512]{1,0:T(8,128)(2,1)}, bf16[512,512]{1,0:T(8,128)(2,1)}, u32[]{:S(2)}, u32[]{:S(2)}) collective-permute-start(bf16[512,512]{1,0:T(8,128)(2,1)} %get-tuple-element.16), channel_id=1, source_target_pairs={{0,3},{1,0},{2,1},{3,2},{4,7},{5,4},{6,5},{7,6},{8,11},{9,8},{10,9... | collective-permute-start | bytes 1572872 | tf_op jit(solution)/shard_map/ppermute | solution.py:27
  197.8 12.2 %copy-start.11 = (f32[1152]{0:T(1024)S(1)}, f32[1152]{0:T(1024)}, u32[]{:S(2)}) copy-start(f32[1152]{0:T(1024)} %param.15) | copy-start | bytes 13828
  (9 other events, 33.1 us)
where the time goes:
time: 215 us; the launch traced here: 213 us
  starting transfers between devices  61.4 us (29%)
  waiting for transfers between devices  51.8 us (24%)
  Pallas kernels  38.5 us (18%)
  matrix products  24.9 us (12%)
  other arithmetic  14.9 us (7%)
  local copies, waits for them, and re-layouts  13 us (6%)
  blocking collectives  7.86 us (4%)
    ppermute x8, starting transfers between devices, shifted(): return lax.ppermute(x, axis, pairs)  39.2 us
    pallas_call x1, Pallas kernels, window_attention(): pl.pallas_call(kernel, out_shape=(jax.ShapeDtypeStruct((tok_rows, local_k...  38.5 us
    ppermute x6, waiting for transfers between devices, cyclic(): lax.ppermute(x, axis, [(i, (i + by) % devices) for i in range(devices)])  31.3 us
    ppermute x8, waiting for transfers between devices, shifted(): return lax.ppermute(x, axis, pairs)  11.3 us
    ppermute x5, starting transfers between devices, from_first(): got = lax.ppermute(x, axis, pairs)  11.1 us
    ppermute x6, starting transfers between devices, cyclic(): lax.ppermute(x, axis, [(i, (i + by) % devices) for i in range(devices)])  11.1 us
    ppermute x5, waiting for transfers between devices, from_first(): got = lax.ppermute(x, axis, pairs)  9.21 us
    psum x1, blocking collectives, on_device(): total_squares, total_sinks = lax.psum((squares, sink_sums), 'tp')  7.86 us
  transfers between devices with their start and end apart: 19, of which 8 were waited for; matrix products, arithmetic and copies ran while one was open for 9% of the time, Pallas kernels for 0%

commit v1 on v0

--- a/solution.py
+++ b/solution.py
@@ -232,11 +232,29 @@
     values = jnp.dot(normed, w_value, preferred_element_type=jnp.float32).astype(jnp.bfloat16)
     kv = jnp.concatenate([keys, values], axis=1)
 
-    sink_kv = from_first(kv[:SINKS], "ctx")
+    sink_rows = from_first(hidden_in[:SINKS], "ctx").astype(jnp.float32)
+    sink_normed = (
+        sink_rows * lax.rsqrt(jnp.mean(sink_rows * sink_rows, axis=-1, keepdims=True) + 1e-06) * pre_gain
+    ).astype(jnp.bfloat16)
+    sink_cos, sink_sin = rope_tables(jnp.arange(SINKS, dtype=jnp.int32))
+    sink_keys = jnp.dot(sink_normed, w_key, preferred_element_type=jnp.float32).reshape(SINKS, -1, HEAD)
+    sink_keys = rotate(sink_keys, sink_cos, sink_sin).astype(jnp.bfloat16).reshape(SINKS, -1)
+    sink_values = jnp.dot(sink_normed, w_value, preferred_element_type=jnp.float32).astype(jnp.bfloat16)
+    sink_kv = jnp.concatenate([sink_keys, sink_values], axis=1)
     sink_pad = jnp.zeros((HEAD, sink_kv.shape[1]), sink_kv.dtype).at[:SINKS].set(sink_kv)
     reach = WINDOW // tok_rows
-    pieces = [shifted(kv, "ctx", distance) for distance in range(reach, 0, -1)] + [kv]
-    orders = (tuple(range(len(pieces))),)
+    ctx_n = lax.axis_size("ctx")
+    fetched = [shifted(kv, "ctx", distance) for distance in range(reach, 0, -2)]
+    swap_pairs = [(i, i ^ 1) for i in range(ctx_n)]
+    swapped = [lax.ppermute(x, "ctx", swap_pairs) for x in fetched + [kv]]
+    pieces = fetched + swapped + [kv]
+    own = len(pieces) - 1
+    half = len(fetched)
+    even_order, odd_order = [], []
+    for j in range(half):
+        even_order += [j, half + j]
+        odd_order += [j, half + j + 1]
+    orders = (tuple(even_order + [own]), tuple(odd_order + [own]))
     attended, sink_parts = window_attention(
         query, cosine_table[:, 0, :], sine_table[:, 0, :], pieces, orders, sink_pad, offset, local_kv, group,
         extra=tuple(w_recv[1:]),

time: 215 us -> 207 us (0.963)
  the two profiles are of different devices: /device:TPU:8 before, /device:TPU:114 now
where the time goes in v1:
time: 207 us; the launch traced here: 206 us
  waiting for transfers between devices  77.8 us (38%)
  Pallas kernels  38.6 us (19%)
  starting transfers between devices  26.6 us (13%)
  matrix products  26 us (13%)
  other arithmetic  15 us (7%)
  local copies, waits for them, and re-layouts  10.7 us (5%)
  blocking collectives  10.5 us (5%)
    ppermute x6, waiting for transfers between devices, cyclic(): lax.ppermute(x, axis, [(i, (i + by) % devices) for i in range(devices)])  61.1 us
    pallas_call x1, Pallas kernels, window_attention(): pl.pallas_call(kernel, out_shape=(jax.ShapeDtypeStruct((tok_rows, local_k...  38.6 us
    ppermute x5, waiting for transfers between devices, from_first(): got = lax.ppermute(x, axis, pairs)  14.7 us
    ppermute x4, starting transfers between devices, shifted(): return lax.ppermute(x, axis, pairs)  11.6 us
    psum x1, blocking collectives, on_device(): total_squares, total_sinks = lax.psum((squares, sink_sums), 'tp')  10.5 us
    ppermute x6, starting transfers between devices, cyclic(): lax.ppermute(x, axis, [(i, (i + by) % devices) for i in range(devices)])  9.26 us
    dot_general x3, matrix products, on_device(): jnp.dot(cyclic(attended, 'tp', k), w_recv[k], preferred_element_type=jnp....  6.5 us
    dot_general x1, matrix products, on_device(): query = jnp.dot(normed, w_query, preferred_element_type=jnp.float32)  5.98 us
  transfers between devices with their start and end apart: 20, of which 11 were waited for; matrix products, arithmetic and copies ran while one was open for 10% of the time, Pallas kernels for 0%

profile of v1, /device:TPU:114, one launch (start us, length us, event | category | flops | bytes accessed | tf_op | source)
XLA Modules:
  0.0 206.2 jit_solution(12935594220265196666)
XLA Ops:
  2.0 3.6 %fusion = f32[512]{0:T(512)S(1)} fusion(bf16[512,4608]{1,0:T(8,128)(2,1)} %param.9), kind=kLoop, calls=%fused_computation.2 | loop fusion | flops 7077376 | bytes 4720640 | tf_op jit(solution)/shard_map/reduce_sum | solution.py:225
  11.8 2.0 copy.15
  13.8 4.7 %convolution_convert_fusion = bf16[512,256]{1,0:T(8,128)(2,1)S(1)} fusion(bf16[4608,256]{1,0:T(8,128)(2,1)} %param.13, bf16[512,4608]{1,0:T(8,128)(2,1)} %param.9, f32[4608]{0:T(1024)S(1)} %copy-done.14, f32[512]{0:T(512)S(1)} %add_rsqrt_fusion.1), kind=kOutput, calls=%fused_computation.10 | convolution fusion | flops 1217527808 | bytes 7360512 | tf_op jit(solution)/shard_map/dot_general | solution.py:232
  20.5 3.0 %collective-permute-start.6 = (bf16[512,512]{1,0:T(8,128)(2,1)}, bf16[512,512]{1,0:T(8,128)(2,1)S(1)}, u32[]{:S(2)}, u32[]{:S(2)}) collective-permute-start(bf16[512,512]{1,0:T(8,128)(2,1)} %pad_maximum_fusion.rest_9_), channel_id=1, source_target_pairs={{0,24},{4,28},{8,32},{12,36},{16,40},{20,44},{24,48},{28,52},{32,5... | collective-permute-start | bytes 1572872 | tf_op jit(solution)/shard_map/ppermute | solution.py:22
  23.5 1.9 collective-permute-start.7
  25.5 4.7 %collective-permute-start.8 = (bf16[512,512]{1,0:T(8,128)(2,1)}, bf16[512,512]{1,0:T(8,128)(2,1)}, u32[]{:S(2)}, u32[]{:S(2)}) collective-permute-start(bf16[512,512]{1,0:T(8,128)(2,1)} %pad_maximum_fusion.rest_9_), channel_id=1, source_target_pairs={{0,8},{4,12},{8,16},{12,20},{16,24},{20,28},{24,32},{28,36},{32,40... | collective-permute-start | bytes 1572872 | tf_op jit(solution)/shard_map/ppermute | solution.py:22
  30.2 1.9 collective-permute-start.5
  32.9 6.0 %fusion.26.q_ref = f32[512,512]{1,0:T(8,128)} fusion(bf16[4608,512]{1,0:T(8,128)(2,1)} %param.11, bf16[512,4608]{1,0:T(8,128)(2,1)S(1)} %bitcast.37, f32[4608]{0:T(1024)S(1)} %copy-done.14, f32[512]{0:T(512)S(1)} %add_rsqrt_fusion.1), kind=kOutput, calls=%fused_computation.60 | convolution fusion | flops 2425356288 | bytes 10506240 | tf_op jit(solution)/shard_map/dot_general | solution.py:229
  40.4 3.9 %constant_dynamic-slice_fusion = (bf16[512,1152]{1,0:T(8,128)(2,1)}, bf16[512,1152]{1,0:T(8,128)(2,1)}, bf16[512,1152]{1,0:T(8,128)(2,1)}) fusion(bf16[512,4608]{1,0:T(8,128)(2,1)} %param.14, s32[]{:T(128)S(6)} %select_n.107, s32[]{:T(128)S(6)} %select_n.105, s32[]{:T(128)S(6)} %select_n.103), kind=kLoop, calls=%fused_computation.51 | loop fusion | bytes 7077900 | tf_op jit(solution)/shard_map/dynamic_slice | solution.py:219
  46.4 14.0 %collective-permute-done.3 = bf16[4,4608]{1,0:T(4,128)(2,1)S(1)} collective-permute-done((bf16[4,4608]{1,0:T(4,128)(2,1)S(1)}, bf16[4,4608]{1,0:T(4,128)(2,1)S(1)}, u32[]{:S(2)}, u32[]{:S(2)}) %collective-permute-start.3) | collective-permute-done | bytes 36896 | tf_op jit(solution)/shard_map/ppermute | solution.py:36
  66.6 2.1 %collective-permute-start.16 = (bf16[512,1152]{1,0:T(8,128)(2,1)}, bf16[512,1152]{1,0:T(8,128)(2,1)}, u32[]{:S(2)}, u32[]{:S(2)}) collective-permute-start(bf16[512,1152]{1,0:T(8,128)(2,1)} %get-tuple-element.20), channel_id=1, source_target_pairs={{0,3},{1,0},{2,1},{3,2},{4,7},{5,4},{6,5},{7,6},{8,11},{9,8},{10,9... | collective-permute-start | bytes 3538952 | tf_op jit(solution)/shard_map/ppermute | solution.py:27
  73.1 2.2 %convolution_convert_fusion.1 = bf16[4,256]{1,0:T(4,128)(2,1)S(1)} fusion(bf16[4608,256]{1,0:T(8,128)(2,1)} %param.13, f32[4608]{0:T(1024)} %param.10, f32[4]{0:T(128)} %copy-done.16, bf16[4,4608]{1,0:T(4,128)(2,1)} %copy-done.13, bf16[4,4608]{1,0:T(4,128)(2,1)} %copy-done.8, pred[]{:T(512)S(6)} %eq.25), kind=kOutput, calls=%fused_computation.12 | convolution fusion | flops 9530368 | bytes 2453521 | tf_op jit(solution)/shard_map/dot_general | solution.py:242
  75.9 17.2 %collective-permute-done.14.rest_10_ = bf16[512,1152]{1,0:T(8,128)(2,1)S(1)} collective-permute-done((bf16[512,1152]{1,0:T(8,128)(2,1)}, bf16[512,1152]{1,0:T(8,128)(2,1)S(1)}, u32[]{:S(2)}, u32[]{:S(2)}) %collective-permute-start.14) | collective-permute-done | bytes 1179680 | tf_op jit(solution)/shard_map/ppermute | solution.py:27
  93.1 3.1 %collective-permute-done.15.rest_11_ = bf16[512,1152]{1,0:T(8,128)(2,1)} collective-permute-done((bf16[512,1152]{1,0:T(8,128)(2,1)}, bf16[512,1152]{1,0:T(8,128)(2,1)}, u32[]{:S(2)}, u32[]{:S(2)}) %collective-permute-start.15) | collective-permute-done | bytes 1179680 | tf_op jit(solution)/shard_map/ppermute | solution.py:27
  96.2 23.7 %collective-permute-done.16.rest_12_ = bf16[512,1152]{1,0:T(8,128)(2,1)} collective-permute-done((bf16[512,1152]{1,0:T(8,128)(2,1)}, bf16[512,1152]{1,0:T(8,128)(2,1)}, u32[]{:S(2)}, u32[]{:S(2)}) %collective-permute-start.16) | collective-permute-done | bytes 1179680 | tf_op jit(solution)/shard_map/ppermute | solution.py:27
  119.9 38.6 %shard_map.86 = (bf16[512,512]{1,0:T(8,128)(2,1)}, f32[2,2,512,1]{3,2,1,0:T(8,128)}) custom-call(s32[1]{0:T(128)} %bitcast.off_ref, f32[512,512]{1,0:T(8,128)} %fusion.26.q_ref, f32[512,128]{1,0:T(8,128)} %copy-done.4, f32[512,128]{1,0:T(8,128)} %copy-done.3, bf16[128,512]{1,0:T(8,128)(2,1)} %fusion.11.sk_ref.sv_ref, bf16[128,512]{1,0:T(8,128)(2,1)} %fusion.11.sk_ref.sv_ref, ...), custom_call_target="tpu_custom_call" | custom-call | tf_op jit(solution)/shard_map/pallas_call | solution.py:174
  164.4 9.2 %collective-permute-done.17 = bf16[512,512]{1,0:T(8,128)(2,1)S(1)} collective-permute-done((bf16[512,512]{1,0:T(8,128)(2,1)}, bf16[512,512]{1,0:T(8,128)(2,1)S(1)}, u32[]{:S(2)}, u32[]{:S(2)}) %collective-permute-start.17) | collective-permute-done | bytes 524320 | tf_op jit(solution)/shard_map/ppermute | solution.py:27
  173.6 2.1 %fusion.29 = f32[512,1152]{1,0:T(8,128)S(1)} fusion(bf16[512,512]{1,0:T(8,128)(2,1)S(1)} %collective-permute-done.17, bf16[512,1152]{1,0:T(8,128)(2,1)} %copy-done.2), kind=kOutput, calls=%fused_computation.62 | convolution fusion | flops 603979776 | bytes 4063232 | tf_op jit(solution)/shard_map/dot_general | solution.py:265
  176.4 2.1 %fusion.30 = f32[512,1152]{1,0:T(8,128)S(1)} fusion(bf16[512,512]{1,0:T(8,128)(2,1)S(1)} %collective-permute-done.18, bf16[512,1152]{1,0:T(8,128)(2,1)} %collective-permute-done.15.rest_11_), kind=kOutput, calls=%fused_computation.63 | convolution fusion | flops 603979776 | bytes 4063232 | tf_op jit(solution)/shard_map/dot_general | solution.py:265
  178.5 7.1 %collective-permute-done.19 = bf16[512,512]{1,0:T(8,128)(2,1)} collective-permute-done((bf16[512,512]{1,0:T(8,128)(2,1)}, bf16[512,512]{1,0:T(8,128)(2,1)}, u32[]{:S(2)}, u32[]{:S(2)}) %collective-permute-start.19) | collective-permute-done | bytes 524320 | tf_op jit(solution)/shard_map/ppermute | solution.py:27
  185.7 2.3 %fusion.31 = f32[512,1152]{1,0:T(8,128)S(1)} fusion(bf16[512,512]{1,0:T(8,128)(2,1)} %collective-permute-done.19, bf16[512,1152]{1,0:T(8,128)(2,1)} %collective-permute-done.16.rest_12_), kind=kOutput, calls=%fused_computation.64 | convolution fusion | flops 603979776 | bytes 4063232 | tf_op jit(solution)/shard_map/dot_general | solution.py:265
  188.0 3.8 %multiply_reduce_fusion = (f32[512]{0:T(512)S(1)}, f32[512,1152]{1,0:T(8,128)}) fusion(f32[512,1152]{1,0:T(8,128)S(1)} %fusion.31, f32[512,1152]{1,0:T(8,128)S(1)} %fusion.30, f32[512,1152]{1,0:T(8,128)S(1)} %fusion.29, bf16[512,512]{1,0:T(8,128)(2,1)S(1)} %copy-done.9, bf16[512,4608]{1,0:T(8,128)(2,1)} %param.14, s32[]{:T(128)S(6)} %select_n.109), kind=kOutput, calls=%fused_computation.9 | convolution fusion | flops 606928384 | bytes 11143172 | tf_op jit(solution)/shard_map/dot_general | solution.py:263
  191.7 10.5 %all-reduce.1 = (f32[512]{0:T(512)S(1)}, f32[512]{0:T(512)S(1)}) all-reduce(f32[512]{0:T(512)S(1)} %get-tuple-element.31, f32[512]{0:T(512)S(1)} %reduce_sum.39), channel_id=1, replica_groups=mesh['ctx'=32,'tp'=4] {'tp'}, use_global_device_ids=true, to_apply=%region_3.4 | all-reduce | flops 1024 | bytes 8192 | tf_op jit(solution)/shard_map/psum | solution.py:269
  202.8 3.4 %add_convert_fusion = bf16[512,1152]{1,0:T(8,128)(2,1)} fusion(f32[512,1152]{1,0:T(8,128)} %get-tuple-element.32, f32[1152]{0:T(1024)S(1)} %copy-done.15, f32[512]{0:T(512)S(1)} %get-tuple-element.34, bf16[512,4608]{1,0:T(8,128)(2,1)} %param.9, s32[]{:T(128)S(6)} %select_n.86), kind=kLoop, calls=%fused_computation.8 | loop fusion | flops 2949120 | bytes 4725252 | tf_op jit(solution)/shard_map/convert_element_type | solution.py:272
  (101 shorter events, 32.2 us)
Async XLA Ops:
  11.8 20.3 %slice-start = ((s8[4718592]{0:T(1024)(128)(4,1)}), s8[524288]{0:T(1024)(128)(4,1)S(1)}, s32[]{:S(2)}) async-start(s8[4718592]{0:T(1024)(128)(4,1)} %bitcast.36), calls=%async_computation | async-start | bytes 1048576
  13.8 18.3 %slice-start.1 = ((s8[4718592]{0:T(1024)(128)(4,1)}), s8[4194304]{0:T(1024)(128)(4,1)S(1)}, s32[]{:S(2)}) async-start(s8[4718592]{0:T(1024)(128)(4,1)} %bitcast.36), calls=%async_computation.1 | async-start | bytes 8388608
  20.5 42.6 %collective-permute-start.6 = (bf16[512,512]{1,0:T(8,128)(2,1)}, bf16[512,512]{1,0:T(8,128)(2,1)S(1)}, u32[]{:S(2)}, u32[]{:S(2)}) collective-permute-start(bf16[512,512]{1,0:T(8,128)(2,1)} %pad_maximum_fusion.rest_9_), channel_id=1, source_target_pairs={{0,24},{4,28},{8,32},{12,36},{16,40},{20,44},{24,48},{28,52},{32,5... | collective-permute-start | bytes 1572872 | tf_op jit(solution)/shard_map/ppermute | solution.py:22
  23.5 42.0 %collective-permute-start.7 = (bf16[512,512]{1,0:T(8,128)(2,1)}, bf16[512,512]{1,0:T(8,128)(2,1)}, u32[]{:S(2)}, u32[]{:S(2)}) collective-permute-start(bf16[512,512]{1,0:T(8,128)(2,1)} %pad_maximum_fusion.rest_9_), channel_id=1, source_target_pairs={{0,16},{4,20},{8,24},{12,28},{16,32},{20,36},{24,40},{28,44},{32,4... | collective-permute-start | bytes 1572872 | tf_op jit(solution)/shard_map/ppermute | solution.py:22
  25.5 41.2 %collective-permute-start.8 = (bf16[512,512]{1,0:T(8,128)(2,1)}, bf16[512,512]{1,0:T(8,128)(2,1)}, u32[]{:S(2)}, u32[]{:S(2)}) collective-permute-start(bf16[512,512]{1,0:T(8,128)(2,1)} %pad_maximum_fusion.rest_9_), channel_id=1, source_target_pairs={{0,8},{4,12},{8,16},{12,20},{16,24},{20,28},{24,32},{28,36},{32,40... | collective-permute-start | bytes 1572872 | tf_op jit(solution)/shard_map/ppermute | solution.py:22
  30.2 39.7 %collective-permute-start.5 = (bf16[512,512]{1,0:T(8,128)(2,1)}, bf16[512,512]{1,0:T(8,128)(2,1)}, u32[]{:S(2)}, u32[]{:S(2)}) collective-permute-start(bf16[512,512]{1,0:T(8,128)(2,1)} %pad_maximum_fusion.rest_9_), channel_id=1, source_target_pairs={{0,32},{4,36},{8,40},{12,44},{16,48},{20,52},{24,56},{28,60},{32,6... | collective-permute-start | bytes 1572872 | tf_op jit(solution)/shard_map/ppermute | solution.py:22
  32.2 6.7 %collective-permute-start = (bf16[4,4608]{1,0:T(4,128)(2,1)S(1)}, bf16[4,4608]{1,0:T(4,128)(2,1)S(1)}, u32[]{:S(2)}, u32[]{:S(2)}) collective-permute-start(bf16[4,4608]{1,0:T(4,128)(2,1)S(1)} %slice.31), channel_id=1, source_target_pairs={{0,64},{1,65},{2,66},{3,67}} | collective-permute-start | bytes 110600 | tf_op jit(solution)/shard_map/ppermute | solution.py:36
  39.8 4.6 %collective-permute-start.1 = (bf16[4,4608]{1,0:T(4,128)(2,1)S(1)}, bf16[4,4608]{1,0:T(4,128)(2,1)S(1)}, u32[]{:S(2)}, u32[]{:S(2)}) collective-permute-start(bf16[4,4608]{1,0:T(4,128)(2,1)S(1)} %broadcast_select_fusion), channel_id=1, source_target_pairs={{0,32},{64,96},{1,33},{65,97},{2,34},{66,98},{3,35},{67,99}} | collective-permute-start | bytes 110600 | tf_op jit(solution)/shard_map/ppermute | solution.py:36
  44.3 0.7 collective-permute-start.2
  45.1 15.3 %collective-permute-start.3 = (bf16[4,4608]{1,0:T(4,128)(2,1)S(1)}, bf16[4,4608]{1,0:T(4,128)(2,1)S(1)}, u32[]{:S(2)}, u32[]{:S(2)}) collective-permute-start(bf16[4,4608]{1,0:T(4,128)(2,1)S(1)} %broadcast_select_fusion.2), channel_id=1, source_target_pairs={{0,8},{16,24},{32,40},{48,56},{64,72},{80,88},{96,104},{112,120},{... | collective-permute-start | bytes 110600 | tf_op jit(solution)/shard_map/ppermute | solution.py:36
  60.4 2.1 %collective-permute-start.4 = (bf16[4,4608]{1,0:T(4,128)(2,1)S(1)}, bf16[4,4608]{1,0:T(4,128)(2,1)S(1)}, u32[]{:S(2)}, u32[]{:S(2)}) collective-permute-start(bf16[4,4608]{1,0:T(4,128)(2,1)S(1)} %broadcast_select_fusion.3), channel_id=1, source_target_pairs={{0,4},{8,12},{16,20},{24,28},{32,36},{40,44},{48,52},{56,60},{64,6... | collective-permute-start | bytes 110600 | tf_op jit(solution)/shard_map/ppermute | solution.py:36
  62.6 7.3 %collective-permute-start.13 = (bf16[512,512]{1,0:T(8,128)(2,1)}, bf16[512,512]{1,0:T(8,128)(2,1)}, u32[]{:S(2)}, u32[]{:S(2)}) collective-permute-start(bf16[512,512]{1,0:T(8,128)(2,1)} %pad_maximum_fusion.rest_9_), channel_id=1, source_target_pairs={{0,4},{4,0},{8,12},{12,8},{16,20},{20,16},{24,28},{28,24},{32,36},... | collective-permute-start | bytes 1572872 | tf_op jit(solution)/shard_map/ppermute | solution.py:249
  64.0 29.1 %collective-permute-start.14 = (bf16[512,1152]{1,0:T(8,128)(2,1)}, bf16[512,1152]{1,0:T(8,128)(2,1)S(1)}, u32[]{:S(2)}, u32[]{:S(2)}) collective-permute-start(bf16[512,1152]{1,0:T(8,128)(2,1)} %get-tuple-element.22), channel_id=1, source_target_pairs={{0,1},{1,2},{2,3},{3,0},{4,5},{5,6},{6,7},{7,4},{8,9},{9,10},{10,1... | collective-permute-start | bytes 3538952 | tf_op jit(solution)/shard_map/ppermute | solution.py:27
  65.5 30.7 %collective-permute-start.15 = (bf16[512,1152]{1,0:T(8,128)(2,1)}, bf16[512,1152]{1,0:T(8,128)(2,1)}, u32[]{:S(2)}, u32[]{:S(2)}) collective-permute-start(bf16[512,1152]{1,0:T(8,128)(2,1)} %get-tuple-element.21), channel_id=1, source_target_pairs={{0,2},{1,3},{2,0},{3,1},{4,6},{5,7},{6,4},{7,5},{8,10},{9,11},{10,... | collective-permute-start | bytes 3538952 | tf_op jit(solution)/shard_map/ppermute | solution.py:27
  66.6 53.3 %collective-permute-start.16 = (bf16[512,1152]{1,0:T(8,128)(2,1)}, bf16[512,1152]{1,0:T(8,128)(2,1)}, u32[]{:S(2)}, u32[]{:S(2)}) collective-permute-start(bf16[512,1152]{1,0:T(8,128)(2,1)} %get-tuple-element.20), channel_id=1, source_target_pairs={{0,3},{1,0},{2,1},{3,2},{4,7},{5,4},{6,5},{7,6},{8,11},{9,8},{10,9... | collective-permute-start | bytes 3538952 | tf_op jit(solution)/shard_map/ppermute | solution.py:27
  69.9 2.3 %collective-permute-start.10 = (bf16[512,512]{1,0:T(8,128)(2,1)}, bf16[512,512]{1,0:T(8,128)(2,1)}, u32[]{:S(2)}, u32[]{:S(2)}) collective-permute-start(bf16[512,512]{1,0:T(8,128)(2,1)} %copy-done.10), channel_id=1, source_target_pairs={{0,4},{4,0},{8,12},{12,8},{16,20},{20,16},{24,28},{28,24},{32,36},... | collective-permute-start | bytes 1572872 | tf_op jit(solution)/shard_map/ppermute | solution.py:249
  69.9 3.0 %collective-permute-start.11 = (bf16[512,512]{1,0:T(8,128)(2,1)}, bf16[512,512]{1,0:T(8,128)(2,1)}, u32[]{:S(2)}, u32[]{:S(2)}) collective-permute-start(bf16[512,512]{1,0:T(8,128)(2,1)} %collective-permute-done.7.rest_2_), channel_id=1, source_target_pairs={{0,4},{4,0},{8,12},{12,8},{16,20},{20,16},{24,28},{28,24},{32,36},... | collective-permute-start | bytes 1572872 | tf_op jit(solution)/shard_map/ppermute | solution.py:249
  72.2 3.7 %collective-permute-start.12 = (bf16[512,512]{1,0:T(8,128)(2,1)}, bf16[512,512]{1,0:T(8,128)(2,1)S(1)}, u32[]{:S(2)}, u32[]{:S(2)}) collective-permute-start(bf16[512,512]{1,0:T(8,128)(2,1)} %collective-permute-done.8.rest_3_), channel_id=1, source_target_pairs={{0,4},{4,0},{8,12},{12,8},{16,20},{20,16},{24,28},{28,24},{32,36},... | collective-permute-start | bytes 1572872 | tf_op jit(solution)/shard_map/ppermute | solution.py:249
  72.9 3.0 %collective-permute-start.9 = (bf16[512,512]{1,0:T(8,128)(2,1)}, bf16[512,512]{1,0:T(8,128)(2,1)S(1)}, u32[]{:S(2)}, u32[]{:S(2)}) collective-permute-start(bf16[512,512]{1,0:T(8,128)(2,1)} %collective-permute-done.5.rest_0_), channel_id=1, source_target_pairs={{0,4},{4,0},{8,12},{12,8},{16,20},{20,16},{24,28},{28,24},{32,36},... | collective-permute-start | bytes 1572872 | tf_op jit(solution)/shard_map/ppermute | solution.py:249
  75.9 20.3 %copy-start.12 = (bf16[512,512]{1,0:T(8,128)(2,1)}, bf16[512,512]{1,0:T(8,128)(2,1)S(1)}, u32[]{:S(2)}) copy-start(bf16[512,512]{1,0:T(8,128)(2,1)S(1)} %collective-permute-done.9.rest_4_) | copy-start | bytes 1572868
  93.1 26.8 %copy-start.2 = (bf16[512,1152]{1,0:T(8,128)(2,1)}, bf16[512,1152]{1,0:T(8,128)(2,1)S(1)}, u32[]{:S(2)}) copy-start(bf16[512,1152]{1,0:T(8,128)(2,1)S(1)} %collective-permute-done.14.rest_10_) | copy-start | bytes 3538948
  158.5 15.1 %collective-permute-start.17 = (bf16[512,512]{1,0:T(8,128)(2,1)}, bf16[512,512]{1,0:T(8,128)(2,1)S(1)}, u32[]{:S(2)}, u32[]{:S(2)}) collective-permute-start(bf16[512,512]{1,0:T(8,128)(2,1)} %get-tuple-element.16), channel_id=1, source_target_pairs={{0,1},{1,2},{2,3},{3,0},{4,5},{5,6},{6,7},{7,4},{8,9},{9,10},{10,1... | collective-permute-start | bytes 1572872 | tf_op jit(solution)/shard_map/ppermute | solution.py:27
  159.9 16.5 %collective-permute-start.18 = (bf16[512,512]{1,0:T(8,128)(2,1)}, bf16[512,512]{1,0:T(8,128)(2,1)S(1)}, u32[]{:S(2)}, u32[]{:S(2)}) collective-permute-start(bf16[512,512]{1,0:T(8,128)(2,1)} %get-tuple-element.16), channel_id=1, source_target_pairs={{0,2},{1,3},{2,0},{3,1},{4,6},{5,7},{6,4},{7,5},{8,10},{9,11},{10,... | collective-permute-start | bytes 1572872 | tf_op jit(solution)/shard_map/ppermute | solution.py:27
  161.3 24.4 %collective-permute-start.19 = (bf16[512,512]{1,0:T(8,128)(2,1)}, bf16[512,512]{1,0:T(8,128)(2,1)}, u32[]{:S(2)}, u32[]{:S(2)}) collective-permute-start(bf16[512,512]{1,0:T(8,128)(2,1)} %get-tuple-element.16), channel_id=1, source_target_pairs={{0,3},{1,0},{2,1},{3,2},{4,7},{5,4},{6,5},{7,6},{8,11},{9,8},{10,9... | collective-permute-start | bytes 1572872 | tf_op jit(solution)/shard_map/ppermute | solution.py:27
  (15 other events, 110.9 us)

commit v2 on v1

--- a/solution.py
+++ b/solution.py
@@ -30,12 +30,17 @@
 def from_first(x, axis):
     devices = lax.axis_size(axis)
     index = lax.axis_index(axis)
-    step = devices // 2
-    while step >= 1:
-        pairs = [(i, i + step) for i in range(0, devices, 2 * step)]
-        got = lax.ppermute(x, axis, pairs)
-        x = jnp.where(index % (2 * step) == step, got, x)
-        step //= 2
+    span = devices
+    while span > 1:
+        fan = 4 if span % 4 == 0 else 2
+        stride = span // fan
+        sent = x
+        for k in range(1, fan):
+            pairs = [(i, i + k * stride) for i in range(0, devices, span)]
+            got = lax.ppermute(x, axis, pairs)
+            sent = jnp.where(index % span == k * stride, got, sent)
+        x = sent
+        span = stride
     return x
 
 

time: 207 us -> 211 us (1.019)
  the two profiles are of different devices: /device:TPU:114 before, /device:TPU:8 now
where the time goes in v2:
time: 211 us; the launch traced here: 210 us
  waiting for transfers between devices  62.9 us (30%)
  starting transfers between devices  39.4 us (19%)
  Pallas kernels  38.7 us (18%)
  matrix products  30.8 us (15%)
  other arithmetic  15.9 us (8%)
  local copies, waits for them, and re-layouts  13.2 us (6%)
  blocking collectives  7.88 us (4%)
    ppermute x6, waiting for transfers between devices, cyclic(): lax.ppermute(x, axis, [(i, (i + by) % devices) for i in range(devices)])  53.4 us
    pallas_call x1, Pallas kernels, window_attention(): pl.pallas_call(kernel, out_shape=(jax.ShapeDtypeStruct((tok_rows, local_k...  38.7 us
    ppermute x4, starting transfers between devices, shifted(): return lax.ppermute(x, axis, pairs)  16.5 us
    ppermute x6, starting transfers between devices, cyclic(): lax.ppermute(x, axis, [(i, (i + by) % devices) for i in range(devices)])  12.3 us
    ppermute x7, starting transfers between devices, from_first(): got = lax.ppermute(x, axis, pairs)  9.5 us
    ppermute x4, waiting for transfers between devices, shifted(): return lax.ppermute(x, axis, pairs)  7.9 us
    psum x1, blocking collectives, on_device(): total_squares, total_sinks = lax.psum((squares, sink_sums), 'tp')  7.88 us
    dot_general x1, matrix products, on_device(): query = jnp.dot(normed, w_query, preferred_element_type=jnp.float32)  7.44 us
  transfers between devices with their start and end apart: 22, of which 9 were waited for; matrix products, arithmetic and copies ran while one was open for 23% of the time, Pallas kernels for 0%

profile of v2, /device:TPU:8, one launch (start us, length us, event | category | flops | bytes accessed | tf_op | source)
XLA Modules:
  0.0 209.8 jit_solution(11238537817643417630)
XLA Ops:
  4.4 3.3 %fusion = f32[512]{0:T(512)S(1)} fusion(bf16[512,4608]{1,0:T(8,128)(2,1)} %param.9), kind=kLoop, calls=%fused_computation.2 | loop fusion | flops 7077376 | bytes 4720640 | tf_op jit(solution)/shard_map/reduce_sum | solution.py:230
  9.0 5.0 %fusion.24 = f32[512,256]{0,1:T(8,128)} fusion(bf16[4608,256]{1,0:T(8,128)(2,1)S(1)} %copy-done, bf16[512,4608]{1,0:T(8,128)(2,1)} %param.9, f32[4608]{0:T(1024)S(1)} %copy-done.12, f32[512]{0:T(512)S(1)} %add_rsqrt_fusion.1), kind=kOutput, calls=%fused_computation.57 | convolution fusion | flops 1217396736 | bytes 7622656 | tf_op jit(solution)/shard_map/dot_general | solution.py:235
  23.2 4.6 %convolution_convert_fusion = bf16[512,256]{1,0:T(8,128)(2,1)S(1)} fusion(bf16[4608,256]{1,0:T(8,128)(2,1)} %param.13, bf16[512,4608]{1,0:T(8,128)(2,1)} %param.9, f32[4608]{0:T(1024)S(1)} %copy-done.12, f32[512]{0:T(512)S(1)} %add_rsqrt_fusion.1), kind=kOutput, calls=%fused_computation.10 | convolution fusion | flops 1217527808 | bytes 7360512 | tf_op jit(solution)/shard_map/dot_general | solution.py:237
  29.7 4.1 %collective-permute-start.7 = (bf16[512,512]{1,0:T(8,128)(2,1)}, bf16[512,512]{1,0:T(8,128)(2,1)S(1)}, u32[]{:S(2)}, u32[]{:S(2)}) collective-permute-start(bf16[512,512]{1,0:T(8,128)(2,1)} %pad_maximum_fusion.rest_9_), channel_id=1, source_target_pairs={{0,32},{4,36},{8,40},{12,44},{16,48},{20,52},{24,56},{28,60},{32,6... | collective-permute-start | bytes 1572872 | tf_op jit(solution)/shard_map/ppermute | solution.py:22
  33.7 5.3 %collective-permute-start.8 = (bf16[512,512]{1,0:T(8,128)(2,1)}, bf16[512,512]{1,0:T(8,128)(2,1)}, u32[]{:S(2)}, u32[]{:S(2)}) collective-permute-start(bf16[512,512]{1,0:T(8,128)(2,1)} %pad_maximum_fusion.rest_9_), channel_id=1, source_target_pairs={{0,24},{4,28},{8,32},{12,36},{16,40},{20,44},{24,48},{28,52},{32,5... | collective-permute-start | bytes 1572872 | tf_op jit(solution)/shard_map/ppermute | solution.py:22
  39.1 7.4 %fusion.26.q_ref = f32[512,512]{1,0:T(8,128)} fusion(bf16[4608,512]{1,0:T(8,128)(2,1)} %param.11, bf16[512,4608]{1,0:T(8,128)(2,1)} %param.9, f32[4608]{0:T(1024)S(1)} %copy-done.12, f32[512]{0:T(512)S(1)} %add_rsqrt_fusion.1), kind=kOutput, calls=%fused_computation.58 | convolution fusion | flops 2425356288 | bytes 10506240 | tf_op jit(solution)/shard_map/dot_general | solution.py:234
  46.5 3.9 %constant_dynamic-slice_fusion = (bf16[512,1152]{1,0:T(8,128)(2,1)}, bf16[512,1152]{1,0:T(8,128)(2,1)}, bf16[512,1152]{1,0:T(8,128)(2,1)}) fusion(bf16[512,4608]{1,0:T(8,128)(2,1)} %param.14, s32[]{:T(128)S(6)} %select_n.121, s32[]{:T(128)S(6)} %select_n.119, s32[]{:T(128)S(6)} %select_n.117), kind=kLoop, calls=%fused_computation.49 | loop fusion | bytes 7077900 | tf_op jit(solution)/shard_map/dynamic_slice | solution.py:224
  51.4 3.0 %collective-permute-start.3 = (bf16[4,4608]{1,0:T(4,128)(2,1)S(1)}, bf16[4,4608]{1,0:T(4,128)(2,1)S(1)}, u32[]{:S(2)}, u32[]{:S(2)}) collective-permute-start(bf16[4,4608]{1,0:T(4,128)(2,1)S(1)} %select_select_fusion.1), channel_id=1, source_target_pairs={{0,24},{32,56},{64,88},{96,120},{1,25},{33,57},{65,89},{97,121},{2... | collective-permute-start | bytes 110600 | tf_op jit(solution)/shard_map/ppermute | solution.py:40
  59.0 5.2 %collective-permute-start.10 = (bf16[512,512]{1,0:T(8,128)(2,1)}, bf16[512,512]{1,0:T(8,128)(2,1)}, u32[]{:S(2)}, u32[]{:S(2)}) collective-permute-start(bf16[512,512]{1,0:T(8,128)(2,1)} %pad_maximum_fusion.rest_9_), channel_id=1, source_target_pairs={{0,8},{4,12},{8,16},{12,20},{16,24},{20,28},{24,32},{28,36},{32,40... | collective-permute-start | bytes 1572872 | tf_op jit(solution)/shard_map/ppermute | solution.py:22
  69.4 2.7 %collective-permute-start.17 = (bf16[512,1152]{1,0:T(8,128)(2,1)}, bf16[512,1152]{1,0:T(8,128)(2,1)}, u32[]{:S(2)}, u32[]{:S(2)}) collective-permute-start(bf16[512,1152]{1,0:T(8,128)(2,1)} %get-tuple-element.21), channel_id=1, source_target_pairs={{0,2},{1,3},{2,0},{3,1},{4,6},{5,7},{6,4},{7,5},{8,10},{9,11},{10,... | collective-permute-start | bytes 3538952 | tf_op jit(solution)/shard_map/ppermute | solution.py:27
  73.4 2.8 %collective-permute-start.18 = (bf16[512,1152]{1,0:T(8,128)(2,1)}, bf16[512,1152]{1,0:T(8,128)(2,1)}, u32[]{:S(2)}, u32[]{:S(2)}) collective-permute-start(bf16[512,1152]{1,0:T(8,128)(2,1)} %get-tuple-element.20), channel_id=1, source_target_pairs={{0,3},{1,0},{2,1},{3,2},{4,7},{5,4},{6,5},{7,6},{8,11},{9,8},{10,9... | collective-permute-start | bytes 3538952 | tf_op jit(solution)/shard_map/ppermute | solution.py:27
  76.2 6.6 %collective-permute-done.10.rest_3_ = bf16[512,512]{1,0:T(8,128)(2,1)} collective-permute-done((bf16[512,512]{1,0:T(8,128)(2,1)}, bf16[512,512]{1,0:T(8,128)(2,1)}, u32[]{:S(2)}, u32[]{:S(2)}) %collective-permute-start.10) | collective-permute-done | bytes 524320 | tf_op jit(solution)/shard_map/ppermute | solution.py:22
  86.0 2.2 %convolution_convert_fusion.1 = bf16[4,256]{1,0:T(4,128)(2,1)S(1)} fusion(bf16[4608,256]{1,0:T(8,128)(2,1)} %param.13, f32[4608]{0:T(1024)} %param.10, f32[4]{0:T(128)} %copy-done.14, bf16[4,4608]{1,0:T(4,128)(2,1)} %copy-done.11, bf16[4,4608]{1,0:T(4,128)(2,1)} %copy-done.6, pred[]{:T(512)S(6)} %eq.33), kind=kOutput, calls=%fused_computation.12 | convolution fusion | flops 9530368 | bytes 2453521 | tf_op jit(solution)/shard_map/dot_general | solution.py:247
  88.8 8.8 %collective-permute-done.16.rest_10_ = bf16[512,1152]{1,0:T(8,128)(2,1)S(1)} collective-permute-done((bf16[512,1152]{1,0:T(8,128)(2,1)}, bf16[512,1152]{1,0:T(8,128)(2,1)S(1)}, u32[]{:S(2)}, u32[]{:S(2)}) %collective-permute-start.16) | collective-permute-done | bytes 1179680 | tf_op jit(solution)/shard_map/ppermute | solution.py:27
  97.6 26.4 %collective-permute-done.17.rest_11_ = bf16[512,1152]{1,0:T(8,128)(2,1)} collective-permute-done((bf16[512,1152]{1,0:T(8,128)(2,1)}, bf16[512,1152]{1,0:T(8,128)(2,1)}, u32[]{:S(2)}, u32[]{:S(2)}) %collective-permute-start.17) | collective-permute-done | bytes 1179680 | tf_op jit(solution)/shard_map/ppermute | solution.py:27
  124.0 38.7 %shard_map.86 = (bf16[512,512]{1,0:T(8,128)(2,1)}, f32[2,2,512,1]{3,2,1,0:T(8,128)}) custom-call(s32[1]{0:T(128)} %bitcast.off_ref, f32[512,512]{1,0:T(8,128)} %fusion.26.q_ref, f32[512,128]{1,0:T(8,128)} %copy-done.3, f32[512,128]{1,0:T(8,128)} %copy-done.2, bf16[128,512]{1,0:T(8,128)(2,1)} %fusion.11.sk_ref.sv_ref, bf16[128,512]{1,0:T(8,128)(2,1)} %fusion.11.sk_ref.sv_ref, ...), custom_call_target="tpu_custom_call" | custom-call | tf_op jit(solution)/shard_map/pallas_call | solution.py:179
  164.0 2.4 %collective-permute-start.20 = (bf16[512,512]{1,0:T(8,128)(2,1)}, bf16[512,512]{1,0:T(8,128)(2,1)S(1)}, u32[]{:S(2)}, u32[]{:S(2)}) collective-permute-start(bf16[512,512]{1,0:T(8,128)(2,1)} %get-tuple-element.16), channel_id=1, source_target_pairs={{0,2},{1,3},{2,0},{3,1},{4,6},{5,7},{6,4},{7,5},{8,10},{9,11},{10,... | collective-permute-start | bytes 1572872 | tf_op jit(solution)/shard_map/ppermute | solution.py:27
  169.3 8.1 %collective-permute-done.19 = bf16[512,512]{1,0:T(8,128)(2,1)S(1)} collective-permute-done((bf16[512,512]{1,0:T(8,128)(2,1)}, bf16[512,512]{1,0:T(8,128)(2,1)S(1)}, u32[]{:S(2)}, u32[]{:S(2)}) %collective-permute-start.19) | collective-permute-done | bytes 524320 | tf_op jit(solution)/shard_map/ppermute | solution.py:27
  179.5 10.1 %collective-permute-done.20 = bf16[512,512]{1,0:T(8,128)(2,1)S(1)} collective-permute-done((bf16[512,512]{1,0:T(8,128)(2,1)}, bf16[512,512]{1,0:T(8,128)(2,1)S(1)}, u32[]{:S(2)}, u32[]{:S(2)}) %collective-permute-start.20) | collective-permute-done | bytes 524320 | tf_op jit(solution)/shard_map/ppermute | solution.py:27
  189.6 2.1 %fusion.30 = f32[512,1152]{1,0:T(8,128)S(1)} fusion(bf16[512,512]{1,0:T(8,128)(2,1)S(1)} %collective-permute-done.20, bf16[512,1152]{1,0:T(8,128)(2,1)} %collective-permute-done.17.rest_11_), kind=kOutput, calls=%fused_computation.61 | convolution fusion | flops 603979776 | bytes 4063232 | tf_op jit(solution)/shard_map/dot_general | solution.py:270
  191.8 2.3 %fusion.31 = f32[512,1152]{1,0:T(8,128)S(1)} fusion(bf16[512,512]{1,0:T(8,128)(2,1)} %collective-permute-done.21, bf16[512,1152]{1,0:T(8,128)(2,1)} %collective-permute-done.18.rest_12_), kind=kOutput, calls=%fused_computation.62 | convolution fusion | flops 603979776 | bytes 4063232 | tf_op jit(solution)/shard_map/dot_general | solution.py:270
  194.1 3.8 %multiply_reduce_fusion = (f32[512]{0:T(512)S(1)}, f32[512,1152]{1,0:T(8,128)}) fusion(f32[512,1152]{1,0:T(8,128)S(1)} %fusion.31, f32[512,1152]{1,0:T(8,128)S(1)} %fusion.30, f32[512,1152]{1,0:T(8,128)S(1)} %fusion.29, bf16[512,512]{1,0:T(8,128)(2,1)S(1)} %copy-done.7, bf16[512,4608]{1,0:T(8,128)(2,1)} %param.14, s32[]{:T(128)S(6)} %select_n.123), kind=kOutput, calls=%fused_computation.9 | convolution fusion | flops 606928384 | bytes 11143172 | tf_op jit(solution)/shard_map/dot_general | solution.py:268
  197.9 7.9 %all-reduce.1 = (f32[512]{0:T(512)S(1)}, f32[512]{0:T(512)S(1)}) all-reduce(f32[512]{0:T(512)S(1)} %get-tuple-element.31, f32[512]{0:T(512)S(1)} %reduce_sum.39), channel_id=1, replica_groups=mesh['ctx'=32,'tp'=4] {'tp'}, use_global_device_ids=true, to_apply=%region_3.4 | all-reduce | flops 1024 | bytes 8192 | tf_op jit(solution)/shard_map/psum | solution.py:274
  206.4 3.4 %add_convert_fusion = bf16[512,1152]{1,0:T(8,128)(2,1)} fusion(f32[512,1152]{1,0:T(8,128)} %get-tuple-element.32, f32[1152]{0:T(1024)S(1)} %copy-done.13, f32[512]{0:T(512)S(1)} %get-tuple-element.34, bf16[512,4608]{1,0:T(8,128)(2,1)} %param.9, s32[]{:T(128)S(6)} %select_n.98), kind=kLoop, calls=%fused_computation.8 | loop fusion | flops 2949120 | bytes 4725252 | tf_op jit(solution)/shard_map/convert_element_type | solution.py:277
  (94 shorter events, 38.6 us)
Async XLA Ops:
  1.7 48.7 %collective-permute-start = (bf16[4,4608]{1,0:T(4,128)(2,1)S(1)}, bf16[4,4608]{1,0:T(4,128)(2,1)S(1)}, u32[]{:S(2)}, u32[]{:S(2)}) collective-permute-start(bf16[4,4608]{1,0:T(4,128)(2,1)S(1)} %slice.31), channel_id=1, source_target_pairs={{0,96},{1,97},{2,98},{3,99}} | collective-permute-start | bytes 110600 | tf_op jit(solution)/shard_map/ppermute | solution.py:40
  2.4 48.1 %collective-permute-start.1 = (bf16[4,4608]{1,0:T(4,128)(2,1)S(1)}, bf16[4,4608]{1,0:T(4,128)(2,1)S(1)}, u32[]{:S(2)}, u32[]{:S(2)}) collective-permute-start(bf16[4,4608]{1,0:T(4,128)(2,1)S(1)} %slice.31), channel_id=1, source_target_pairs={{0,64},{1,65},{2,66},{3,67}} | collective-permute-start | bytes 110600 | tf_op jit(solution)/shard_map/ppermute | solution.py:40
  3.0 47.4 %collective-permute-start.2 = (bf16[4,4608]{1,0:T(4,128)(2,1)S(1)}, bf16[4,4608]{1,0:T(4,128)(2,1)}, u32[]{:S(2)}, u32[]{:S(2)}) collective-permute-start(bf16[4,4608]{1,0:T(4,128)(2,1)S(1)} %slice.31), channel_id=1, source_target_pairs={{0,32},{1,33},{2,34},{3,35}} | collective-permute-start | bytes 110600 | tf_op jit(solution)/shard_map/ppermute | solution.py:40
  29.7 37.3 %collective-permute-start.7 = (bf16[512,512]{1,0:T(8,128)(2,1)}, bf16[512,512]{1,0:T(8,128)(2,1)S(1)}, u32[]{:S(2)}, u32[]{:S(2)}) collective-permute-start(bf16[512,512]{1,0:T(8,128)(2,1)} %pad_maximum_fusion.rest_9_), channel_id=1, source_target_pairs={{0,32},{4,36},{8,40},{12,44},{16,48},{20,52},{24,56},{28,60},{32,6... | collective-permute-start | bytes 1572872 | tf_op jit(solution)/shard_map/ppermute | solution.py:22
  33.7 35.7 %collective-permute-start.8 = (bf16[512,512]{1,0:T(8,128)(2,1)}, bf16[512,512]{1,0:T(8,128)(2,1)}, u32[]{:S(2)}, u32[]{:S(2)}) collective-permute-start(bf16[512,512]{1,0:T(8,128)(2,1)} %pad_maximum_fusion.rest_9_), channel_id=1, source_target_pairs={{0,24},{4,28},{8,32},{12,36},{16,40},{20,44},{24,48},{28,52},{32,5... | collective-permute-start | bytes 1572872 | tf_op jit(solution)/shard_map/ppermute | solution.py:22
  51.4 5.7 %collective-permute-start.3 = (bf16[4,4608]{1,0:T(4,128)(2,1)S(1)}, bf16[4,4608]{1,0:T(4,128)(2,1)S(1)}, u32[]{:S(2)}, u32[]{:S(2)}) collective-permute-start(bf16[4,4608]{1,0:T(4,128)(2,1)S(1)} %select_select_fusion.1), channel_id=1, source_target_pairs={{0,24},{32,56},{64,88},{96,120},{1,25},{33,57},{65,89},{97,121},{2... | collective-permute-start | bytes 110600 | tf_op jit(solution)/shard_map/ppermute | solution.py:40
  54.4 4.6 %collective-permute-start.4 = (bf16[4,4608]{1,0:T(4,128)(2,1)S(1)}, bf16[4,4608]{1,0:T(4,128)(2,1)S(1)}, u32[]{:S(2)}, u32[]{:S(2)}) collective-permute-start(bf16[4,4608]{1,0:T(4,128)(2,1)S(1)} %select_select_fusion.1), channel_id=1, source_target_pairs={{0,16},{32,48},{64,80},{96,112},{1,17},{33,49},{65,81},{97,113},{2... | collective-permute-start | bytes 110600 | tf_op jit(solution)/shard_map/ppermute | solution.py:40
  55.7 8.5 %collective-permute-start.5 = (bf16[4,4608]{1,0:T(4,128)(2,1)S(1)}, bf16[4,4608]{1,0:T(4,128)(2,1)S(1)}, u32[]{:S(2)}, u32[]{:S(2)}) collective-permute-start(bf16[4,4608]{1,0:T(4,128)(2,1)S(1)} %select_select_fusion.1), channel_id=1, source_target_pairs={{0,8},{32,40},{64,72},{96,104},{1,9},{33,41},{65,73},{97,105},{2,1... | collective-permute-start | bytes 110600 | tf_op jit(solution)/shard_map/ppermute | solution.py:40
  57.1 16.3 %collective-permute-start.9 = (bf16[512,512]{1,0:T(8,128)(2,1)}, bf16[512,512]{1,0:T(8,128)(2,1)}, u32[]{:S(2)}, u32[]{:S(2)}) collective-permute-start(bf16[512,512]{1,0:T(8,128)(2,1)} %pad_maximum_fusion.rest_9_), channel_id=1, source_target_pairs={{0,16},{4,20},{8,24},{12,28},{16,32},{20,36},{24,40},{28,44},{32,4... | collective-permute-start | bytes 1572872 | tf_op jit(solution)/shard_map/ppermute | solution.py:22
  59.0 23.8 %collective-permute-start.10 = (bf16[512,512]{1,0:T(8,128)(2,1)}, bf16[512,512]{1,0:T(8,128)(2,1)}, u32[]{:S(2)}, u32[]{:S(2)}) collective-permute-start(bf16[512,512]{1,0:T(8,128)(2,1)} %pad_maximum_fusion.rest_9_), channel_id=1, source_target_pairs={{0,8},{4,12},{8,16},{12,20},{16,24},{20,28},{24,32},{28,36},{32,40... | collective-permute-start | bytes 1572872 | tf_op jit(solution)/shard_map/ppermute | solution.py:22
  64.3 2.1 %collective-permute-start.6 = (bf16[4,4608]{1,0:T(4,128)(2,1)S(1)}, bf16[4,4608]{1,0:T(4,128)(2,1)S(1)}, u32[]{:S(2)}, u32[]{:S(2)}) collective-permute-start(bf16[4,4608]{1,0:T(4,128)(2,1)S(1)} %select_select_fusion), channel_id=1, source_target_pairs={{0,4},{8,12},{16,20},{24,28},{32,36},{40,44},{48,52},{56,60},{64,6... | collective-permute-start | bytes 110600 | tf_op jit(solution)/shard_map/ppermute | solution.py:40
  66.5 16.4 %collective-permute-start.15 = (bf16[512,512]{1,0:T(8,128)(2,1)}, bf16[512,512]{1,0:T(8,128)(2,1)}, u32[]{:S(2)}, u32[]{:S(2)}) collective-permute-start(bf16[512,512]{1,0:T(8,128)(2,1)} %pad_maximum_fusion.rest_9_), channel_id=1, source_target_pairs={{0,4},{4,0},{8,12},{12,8},{16,20},{20,16},{24,28},{28,24},{32,36},... | collective-permute-start | bytes 1572872 | tf_op jit(solution)/shard_map/ppermute | solution.py:254
  67.9 29.6 %collective-permute-start.16 = (bf16[512,1152]{1,0:T(8,128)(2,1)}, bf16[512,1152]{1,0:T(8,128)(2,1)S(1)}, u32[]{:S(2)}, u32[]{:S(2)}) collective-permute-start(bf16[512,1152]{1,0:T(8,128)(2,1)} %get-tuple-element.22), channel_id=1, source_target_pairs={{0,1},{1,2},{2,3},{3,0},{4,5},{5,6},{6,7},{7,4},{8,9},{9,10},{10,1... | collective-permute-start | bytes 3538952 | tf_op jit(solution)/shard_map/ppermute | solution.py:27
  69.4 54.5 %collective-permute-start.17 = (bf16[512,1152]{1,0:T(8,128)(2,1)}, bf16[512,1152]{1,0:T(8,128)(2,1)}, u32[]{:S(2)}, u32[]{:S(2)}) collective-permute-start(bf16[512,1152]{1,0:T(8,128)(2,1)} %get-tuple-element.21), channel_id=1, source_target_pairs={{0,2},{1,3},{2,0},{3,1},{4,6},{5,7},{6,4},{7,5},{8,10},{9,11},{10,... | collective-permute-start | bytes 3538952 | tf_op jit(solution)/shard_map/ppermute | solution.py:27
  73.4 50.5 %collective-permute-start.18 = (bf16[512,1152]{1,0:T(8,128)(2,1)}, bf16[512,1152]{1,0:T(8,128)(2,1)}, u32[]{:S(2)}, u32[]{:S(2)}) collective-permute-start(bf16[512,1152]{1,0:T(8,128)(2,1)} %get-tuple-element.20), channel_id=1, source_target_pairs={{0,3},{1,0},{2,1},{3,2},{4,7},{5,4},{6,5},{7,6},{8,11},{9,8},{10,9... | collective-permute-start | bytes 3538952 | tf_op jit(solution)/shard_map/ppermute | solution.py:27
  82.8 2.3 %collective-permute-start.11 = (bf16[512,512]{1,0:T(8,128)(2,1)}, bf16[512,512]{1,0:T(8,128)(2,1)}, u32[]{:S(2)}, u32[]{:S(2)}) collective-permute-start(bf16[512,512]{1,0:T(8,128)(2,1)} %copy-done.8), channel_id=1, source_target_pairs={{0,4},{4,0},{8,12},{12,8},{16,20},{20,16},{24,28},{28,24},{32,36},... | collective-permute-start | bytes 1572872 | tf_op jit(solution)/shard_map/ppermute | solution.py:254
  82.8 3.0 %collective-permute-start.12 = (bf16[512,512]{1,0:T(8,128)(2,1)}, bf16[512,512]{1,0:T(8,128)(2,1)}, u32[]{:S(2)}, u32[]{:S(2)}) collective-permute-start(bf16[512,512]{1,0:T(8,128)(2,1)} %collective-permute-done.8.rest_1_), channel_id=1, source_target_pairs={{0,4},{4,0},{8,12},{12,8},{16,20},{20,16},{24,28},{28,24},{32,36},... | collective-permute-start | bytes 1572872 | tf_op jit(solution)/shard_map/ppermute | solution.py:254
  85.1 3.7 %collective-permute-start.13 = (bf16[512,512]{1,0:T(8,128)(2,1)}, bf16[512,512]{1,0:T(8,128)(2,1)S(1)}, u32[]{:S(2)}, u32[]{:S(2)}) collective-permute-start(bf16[512,512]{1,0:T(8,128)(2,1)} %collective-permute-done.9.rest_2_), channel_id=1, source_target_pairs={{0,4},{4,0},{8,12},{12,8},{16,20},{20,16},{24,28},{28,24},{32,36},... | collective-permute-start | bytes 1572872 | tf_op jit(solution)/shard_map/ppermute | solution.py:254
  85.8 3.0 %collective-permute-start.14 = (bf16[512,512]{1,0:T(8,128)(2,1)}, bf16[512,512]{1,0:T(8,128)(2,1)S(1)}, u32[]{:S(2)}, u32[]{:S(2)}) collective-permute-start(bf16[512,512]{1,0:T(8,128)(2,1)} %collective-permute-done.10.rest_3_), channel_id=1, source_target_pairs={{0,4},{4,0},{8,12},{12,8},{16,20},{20,16},{24,28},{28,24},{32,36},... | collective-permute-start | bytes 1572872 | tf_op jit(solution)/shard_map/ppermute | solution.py:254
  88.8 35.2 %copy-start.10 = (bf16[512,512]{1,0:T(8,128)(2,1)}, bf16[512,512]{1,0:T(8,128)(2,1)S(1)}, u32[]{:S(2)}) copy-start(bf16[512,512]{1,0:T(8,128)(2,1)S(1)} %collective-permute-done.14.rest_7_) | copy-start | bytes 1572868
  97.6 26.4 %copy-start.1 = (bf16[512,1152]{1,0:T(8,128)(2,1)}, bf16[512,1152]{1,0:T(8,128)(2,1)S(1)}, u32[]{:S(2)}) copy-start(bf16[512,1152]{1,0:T(8,128)(2,1)S(1)} %collective-permute-done.16.rest_10_) | copy-start | bytes 3538948
  162.6 14.8 %collective-permute-start.19 = (bf16[512,512]{1,0:T(8,128)(2,1)}, bf16[512,512]{1,0:T(8,128)(2,1)S(1)}, u32[]{:S(2)}, u32[]{:S(2)}) collective-permute-start(bf16[512,512]{1,0:T(8,128)(2,1)} %get-tuple-element.16), channel_id=1, source_target_pairs={{0,1},{1,2},{2,3},{3,0},{4,5},{5,6},{6,7},{7,4},{8,9},{9,10},{10,1... | collective-permute-start | bytes 1572872 | tf_op jit(solution)/shard_map/ppermute | solution.py:27
  164.0 25.7 %collective-permute-start.20 = (bf16[512,512]{1,0:T(8,128)(2,1)}, bf16[512,512]{1,0:T(8,128)(2,1)S(1)}, u32[]{:S(2)}, u32[]{:S(2)}) collective-permute-start(bf16[512,512]{1,0:T(8,128)(2,1)} %get-tuple-element.16), channel_id=1, source_target_pairs={{0,2},{1,3},{2,0},{3,1},{4,6},{5,7},{6,4},{7,5},{8,10},{9,11},{10,... | collective-permute-start | bytes 1572872 | tf_op jit(solution)/shard_map/ppermute | solution.py:27
  166.4 25.4 %collective-permute-start.21 = (bf16[512,512]{1,0:T(8,128)(2,1)}, bf16[512,512]{1,0:T(8,128)(2,1)}, u32[]{:S(2)}, u32[]{:S(2)}) collective-permute-start(bf16[512,512]{1,0:T(8,128)(2,1)} %get-tuple-element.16), channel_id=1, source_target_pairs={{0,3},{1,0},{2,1},{3,2},{4,7},{5,4},{6,5},{7,6},{8,11},{9,8},{10,9... | collective-permute-start | bytes 1572872 | tf_op jit(solution)/shard_map/ppermute | solution.py:27
  (13 other events, 104.5 us)
